TPU v7x, 128 devices: a whole 4x4x4 slice. The times are simulated.
128 devices in a mesh: wa: 16 (over z, y_hi, core), an: 8 (over y_lo, x).
Axes of the slice: x: 4, y: 4 (y_hi: 2, y_lo: 2; y = y_hi * 2 + y_lo), z: 4, core: 2. Of those that a mesh axis runs over, the one named last changes fastest.
Arguments:
- mass_field: float32 [64, 256, 128, 256], P(None, 'wa', 'an'), may hold values from -8 to 8
- factor_one: float32 [256, 64], replicated, may hold values from -0.375 to 0.375
- factor_two: float32 [256, 64], P('wa'), may hold values from -0.375 to 0.375
- factor_four: float32 [64, 16], replicated, may hold values from -0.75 to 0.75
Outputs:
- gram: float32 [128, 128], P('an')
All inputs are finite; a program needn't handle non-finite values.
Results may differ from a plain program's by a relative error of at most 0.0001.
Values sent between devices are 32-bit elements; how exact they have to be, the bound alone decides.
No kernel may reach another device: no remote copies, remote signals or barrier semaphores. Data moves between devices by JAX's collectives and lax.ppermute only.
A program may use at most 128 MiB of HBM per device.

v0:
```python
import jax
import jax.numpy as jnp
from jax import lax
from jax.sharding import PartitionSpec as P


def on_device(mass_field, factor_one, factor_two, factor_four):
    highest = lax.Precision.HIGHEST
    species_count, fibre_cells, slab_cells, first_cells = mass_field.shape
    rank_one = factor_one.shape[1]
    rank_two = factor_two.shape[1]
    rank_four = factor_four.shape[1]
    reduced = jnp.dot(factor_four.T, mass_field.reshape(species_count, -1), precision=highest)
    reduced = reduced.reshape(rank_four * fibre_cells * slab_cells, first_cells)
    slab_rows = rank_one // lax.axis_size("wa")
    mixed_rows = jnp.dot(reduced, factor_one, precision=highest)
    mixed_rows = mixed_rows.reshape(rank_four, fibre_cells, slab_cells, rank_one)
    term = jnp.einsum("qjkr,jp->rkqp", mixed_rows, factor_two, precision=highest)
    summed = lax.psum(term.reshape(rank_one, slab_cells, rank_four * rank_two), "wa")
    owned_slab = lax.dynamic_slice_in_dim(summed, lax.axis_index("wa") * slab_rows, slab_rows, 0)
    partial_gram = jnp.einsum(
        "rim,rjm->ij",
        owned_slab,
        lax.all_gather(owned_slab, "an", axis=1, tiled=True),
        precision=highest,
    )
    gram_rows = lax.psum(partial_gram, "wa")
    return gram_rows / (rank_one * rank_two * rank_four)


def solution(mesh):
    in_specs = (P(None, "wa", "an", None), P(), P("wa", None), P())
    out_specs = P("an", None)
    return jax.shard_map(
        on_device, mesh=mesh, in_specs=in_specs, out_specs=out_specs, check_vma=False
    )
```

profile of v0, /device:TPU:1, one launch (start us, length us, event | category | flops | bytes accessed | tf_op | source)
XLA Modules:
  0.0 312.5 jit_solution(3219890865373004460)
XLA Ops:
  6.5 0.0 copy-start
  6.5 0.0 all-reduce.2.cloned.1.call-start
  6.5 22.7 %fusion = f32[16,16,16,256]{3,0,2,1:T(8,128)S(1)} fusion(f32[16,16,256,64]{2,1,0,3:T(8,128)} %bitcast.35, f32[64,16]{0,1:T(8,128)} %param.7), kind=kOutput, calls=%fused_computation | convolution fusion | flops 805306368 | bytes 20975616 | tf_op jit(solution)/shard_map/dot_general | solution.py:13
  29.3 0.0 copy-done
  29.3 0.0 copy-start.1
  29.3 5.6 %fusion.2 = f32[16,16,16,64]{3,1,2,0:T(8,128)S(1)} fusion(f32[16,16,16,256]{3,0,2,1:T(8,128)S(1)} %fusion, f32[256,64]{0,1:T(8,128)S(1)} %copy-done), kind=kOutput, calls=%fused_computation.2 | convolution fusion | flops 805306368 | bytes 5308416 | tf_op jit(solution)/shard_map/dot_general | solution.py:16
  34.9 0.0 copy-done.1
  34.9 13.5 %convolution_bitcast_fusion = f32[64,16,16,64]{3,0,1,2:T(8,128)S(1)} fusion(f32[16,16,16,64]{3,1,2,0:T(8,128)S(1)} %fusion.2, f32[16,64]{1,0:T(8,128)S(1)} %copy-done.1), kind=kOutput, calls=%fused_computation.4 | convolution fusion | flops 201326592 | bytes 5246976 | tf_op jit(solution)/shard_map/qjkr,jp->rkqp/dot_general | solution.py:18
  48.4 8.3 %copy.5 = f32[64,16,16,64]{3,2,1,0:T(8,128)} copy(f32[64,16,16,64]{3,0,1,2:T(8,128)S(1)} %convolution_bitcast_fusion) | data formatting | bytes 8388608 | tf_op jit(solution)/shard_map/qjkr,jp->rkqp/transpose | solution.py:18
  56.7 7.6 %reshape.12 = f32[64,16,1024]{2,1,0:T(8,128)} reshape(f32[64,16,16,64]{3,2,1,0:T(8,128)} %copy.5) | data formatting | bytes 8388608 | tf_op jit(solution)/shard_map/reshape | solution.py:19
  64.3 0.0 all-reduce.2.cloned.1.call-update
  64.4 0.0 all-gather.2.cloned.1.call-start
  64.4 158.7 %all-reduce.2.cloned.1.call-done = f32[64,16,1024]{2,1,0:T(8,128)} async-done(((f32[64,16,1024]{2,1,0:T(8,128)}), f32[64,16,1024]{2,1,0:T(8,128)}) %all-reduce.2.cloned.1.call-update) | async-done | bytes 4194320 | tf_op jit(solution)/shard_map/psum | solution.py:19
  223.1 1.7 constant_dynamic-slice_fusion
  224.8 0.0 all-gather.2.cloned.1.call-update
  224.8 38.1 %all-gather.2.cloned.1.call-done = f32[4,128,1024]{2,1,0:T(8,128)} async-done(((f32[4,16,1024]{2,1,0:T(8,128)}), f32[4,128,1024]{2,1,0:T(8,128)}) %all-gather.2.cloned.1.call-update) | async-done | bytes 2097168 | tf_op jit(solution)/shard_map/all_gather | solution.py:24
  262.9 3.4 %convolution_bitcast_fusion.1 = f32[16,128]{1,0:T(8,128)S(1)} fusion(f32[4,16,1024]{2,1,0:T(8,128)} %constant_dynamic-slice_fusion, f32[4,128,1024]{2,1,0:T(8,128)} %all-gather.2.cloned.1.call-done), kind=kOutput, calls=%fused_computation.5 | convolution fusion | flops 100663296 | bytes 2367488 | tf_op jit(solution)/shard_map/rim,rjm->ij/dot_general | solution.py:21
  266.3 38.7 %psum.15 = f32[16,128]{1,0:T(8,128)S(1)} all-reduce(f32[16,128]{1,0:T(8,128)S(1)} %convolution_bitcast_fusion.1), channel_id=1, replica_groups=mesh['wa'=16,'an'=8] {'wa'}, use_global_device_ids=true, to_apply=%region_1.0 | all-reduce | flops 2048 | bytes 16384 | tf_op jit(solution)/shard_map/psum | solution.py:27
  305.0 0.6 broadcast_multiply_fusion
Async XLA Ops:
  6.5 22.7 %copy-start = (f32[256,64]{0,1:T(8,128)S(1)}, f32[256,64]{0,1:T(8,128)}, u32[]{:S(2)}) copy-start(f32[256,64]{0,1:T(8,128)} %param.5) | copy-start | bytes 196612
  6.5 216.6 %all-reduce.2.cloned.1.call-start = ((), (), s32[]{:S(2)}) async-start(), calls=%async_computation | async-start | bytes 8388608 | tf_op jit(solution)/shard_map/psum | solution.py:19
  29.3 5.6 %copy-start.1 = (f32[16,64]{1,0:T(8,128)S(1)}, f32[16,64]{1,0:T(8,128)}, u32[]{:S(2)}) copy-start(f32[16,64]{1,0:T(8,128)} %param.6) | copy-start | bytes 12292
  64.4 198.5 %all-gather.2.cloned.1.call-start = ((), (), s32[]{:S(2)}) async-start(), calls=%async_computation.1 | async-start | bytes 2359296 | tf_op jit(solution)/shard_map/all_gather | solution.py:24
Sparse Core Ops, SparseCore 0:
  64.5 158.5 all-reduce.1
  224.9 37.9 all-gather.1
where the time goes:
time: 313 us; the launch traced here: 312 us
  waiting for transfers between devices  197 us (63%)
  matrix products  45.2 us (14%)
  blocking collectives  38.7 us (12%)
  local copies, waits for them, and re-layouts  17.6 us (6%)
  between operations  13.5 us (4%)
    psum x1, waiting for transfers between devices, on_device(): lax.psum(term.reshape(rank_one, slab_cells, rank_four * rank_two), 'wa')  159 us
    psum x1, blocking collectives, on_device(): gram_rows = lax.psum(partial_gram, 'wa')  38.7 us
    all_gather x1, waiting for transfers between devices, on_device(): lax.all_gather(owned_slab, 'an', axis=1, tiled=True)  38.1 us
    dot_general x1, matrix products, on_device(): jnp.dot(factor_four.T, mass_field.reshape(species_count, -1), precision=h...  22.7 us
    dot_general x1, matrix products, on_device(): jnp.einsum('qjkr,jp->rkqp', mixed_rows, factor_two, precision=highest)  13.5 us
    transpose x1, local copies, waits for them, and re-layouts, on_device(): jnp.einsum('qjkr,jp->rkqp', mixed_rows, factor_two, precision=highest)  8.34 us
    reshape x1, local copies, waits for them, and re-layouts, on_device(): term.reshape(rank_one, slab_cells, rank_four * rank_two)  7.61 us
  transfers between devices with their start and end apart: 2, of which 2 were waited for; matrix products, arithmetic and copies ran while one was open for 0% of the time, Pallas kernels for 0%

commit v1 on v0

v1 whole, which is shorter than its diff:
```python
import jax
import jax.numpy as jnp
from jax import lax
from jax.sharding import PartitionSpec as P


def on_device(mass_field, factor_one, factor_two, factor_four):
    highest = lax.Precision.HIGHEST
    species_count, fibre_cells, slab_cells, first_cells = mass_field.shape
    rank_one = factor_one.shape[1]
    rank_two = factor_two.shape[1]
    rank_four = factor_four.shape[1]
    fibre_parts = lax.axis_size("wa")
    slab_parts = lax.axis_size("an")
    reduced = jnp.dot(factor_four.T, mass_field.reshape(species_count, -1), precision=highest)
    reduced = reduced.reshape(rank_four * fibre_cells * slab_cells, first_cells)
    mixed_rows = jnp.dot(reduced, factor_one, precision=highest)
    mixed_rows = mixed_rows.reshape(rank_four, fibre_cells, slab_cells, rank_one)
    mixed_rows = lax.all_to_all(mixed_rows, "wa", 3, 1, tiled=True)
    whole_two = lax.all_gather(factor_two, "wa", axis=0, tiled=True)
    projected = jnp.einsum("qjkr,jp->rkqp", mixed_rows, whole_two, precision=highest)
    projected = lax.all_to_all(projected, "an", 2, 1, tiled=True)
    partial_gram = jnp.einsum("rkqp,rlqp->kl", projected, projected, precision=highest)
    gram_rows = lax.psum_scatter(partial_gram, "an", scatter_dimension=0, tiled=True)
    gram_rows = lax.psum(gram_rows, "wa")
    return gram_rows / (rank_one * rank_two * rank_four)


def solution(mesh):
    in_specs = (P(None, "wa", "an", None), P(), P("wa", None), P())
    out_specs = P("an", None)
    return jax.shard_map(
        on_device, mesh=mesh, in_specs=in_specs, out_specs=out_specs, check_vma=False
    )
```

time: 313 us -> 203 us (0.65)
  waiting for transfers between devices: 197 us -> 29.1 us
  blocking collectives: 38.7 us -> 80.8 us
  local copies, waits for them, and re-layouts: 17.6 us -> 36.5 us
  matrix products: 45.2 us -> 28.1 us
  starting transfers between devices: 0.04 us -> 9.49 us
  other arithmetic: 0.6 us -> 5.15 us
    psum x1 -> x0, waiting for transfers between devices: 159 us -> none  [on_device(): lax.psum(term.reshape(rank_one, slab_cells, rank_four * rank_two), 'wa')]
    all_gather x1 -> x0, waiting for transfers between devices: 38.1 us -> none  [on_device(): lax.all_gather(owned_slab, 'an', axis=1, tiled=True)]
    all_gather x0 -> x1, blocking collectives: none -> 30.4 us  [on_device(): whole_two = lax.all_gather(factor_two, 'wa', axis=0, tiled=True)]
    reduce_scatter x0 -> x1, waiting for transfers between devices: none -> 29.1 us  [on_device(): lax.psum_scatter(partial_gram, 'an', scatter_dimension=0, tiled=True)]
    all_to_all x0 -> x4, local copies, waits for them, and re-layouts: none -> 16.3 us  [the longest x3 16.3 us: on_device(): mixed_rows = lax.all_to_all(mixed_rows, 'wa', 3, 1, tiled=True)]
    dot_general x2, matrix products: 16.9 us -> 2.18 us  [the longest x1 1.2 us: on_device(): jnp.einsum('rkqp,rlqp->kl', projected, projected, precision=highest)]
    unnamed x4 -> x8, local copies, waits for them, and re-layouts: 0.01 us -> 12.5 us
    all_to_all x0 -> x1, blocking collectives: none -> 11.2 us  [on_device(): projected = lax.all_to_all(projected, 'an', 2, 1, tiled=True)]
  transfers between devices with their start and end apart: 2 -> 2, of which waited for: 2 -> 1; matrix products, arithmetic and copies ran while one was open for 0% -> 0% of each run, Pallas kernels for 0% -> 0%
where the time goes in v1:
time: 203 us
  blocking collectives  80.8 us (40%)
  local copies, waits for them, and re-layouts  36.5 us (18%)
  waiting for transfers between devices  29.1 us (14%)
  matrix products  28.1 us (14%)
  between operations  13.5 us (7%)
  starting transfers between devices  9.49 us (5%)
  other arithmetic  5.15 us (3%)
    psum x1, blocking collectives, on_device(): gram_rows = lax.psum(gram_rows, 'wa')  39.2 us
    all_gather x1, blocking collectives, on_device(): whole_two = lax.all_gather(factor_two, 'wa', axis=0, tiled=True)  30.4 us
    reduce_scatter x1, waiting for transfers between devices, on_device(): lax.psum_scatter(partial_gram, 'an', scatter_dimension=0, tiled=True)  29.1 us
    dot_general x1, matrix products, on_device(): jnp.dot(factor_four.T, mass_field.reshape(species_count, -1), precision=h...  22.5 us
    all_to_all x3, local copies, waits for them, and re-layouts, on_device(): mixed_rows = lax.all_to_all(mixed_rows, 'wa', 3, 1, tiled=True)  16.3 us
    unnamed x8, local copies, waits for them, and re-layouts  12.5 us
    all_to_all x1, blocking collectives, on_device(): projected = lax.all_to_all(projected, 'an', 2, 1, tiled=True)  11.2 us
    all_to_all x1, starting transfers between devices, on_device(): mixed_rows = lax.all_to_all(mixed_rows, 'wa', 3, 1, tiled=True)  9.46 us
  transfers between devices with their start and end apart: 2, of which 1 were waited for; matrix products, arithmetic and copies ran while one was open for 0% of the time, Pallas kernels for 0%

profile of v1, /device:TPU:1, one launch (start us, length us, event | category | flops | bytes accessed | tf_op | source)
XLA Modules:
  0.0 202.7 jit_solution(3701199836332324696)
XLA Ops:
  6.5 0.0 copy-start
  6.5 22.5 %fusion = f32[16,16,16,256]{3,0,2,1:T(8,128)S(1)} fusion(f32[16,16,256,64]{2,1,0,3:T(8,128)} %bitcast.56, f32[64,16]{0,1:T(8,128)} %param.7), kind=kOutput, calls=%fused_computation | convolution fusion | flops 805306368 | bytes 20975616 | tf_op jit(solution)/shard_map/dot_general | solution.py:15
  29.1 0.0 copy-done
  29.1 3.4 %fusion.4 = f32[16,16,16,64]{3,0,2,1:T(8,128)S(1)} fusion(f32[16,16,16,256]{3,0,2,1:T(8,128)S(1)} %fusion, f32[256,64]{0,1:T(8,128)S(1)} %copy-done), kind=kOutput, calls=%fused_computation.6 | convolution fusion | flops 805306368 | bytes 5308416 | tf_op jit(solution)/shard_map/dot_general | solution.py:17
  32.5 7.7 %copy.21 = f32[16,16,16,64]{2,1,0,3:T(8,128)} copy(f32[16,16,16,64]{3,0,2,1:T(8,128)S(1)} %fusion.4) | data formatting | bytes 2097152 | tf_op jit(solution)/shard_map/dot_general | solution.py:17
  40.2 0.0 copy-start.1
  40.2 7.1 %reshape.13 = f32[16,1,16384]{2,1,0:T(1,128)} reshape(f32[64,16,16,16]{3,2,1,0:T(8,128)} %bitcast.54) | data formatting | bytes 2097152
  47.3 9.5 %all-to-all-start = ((f32[16,1,16384]{2,1,0:T(1,128)}), f32[16,1,16384]{2,1,0:T(1,128)S(1)}, u32[]{:S(2)}, u32[]{:S(2)}) async-start(f32[16,1,16384]{2,1,0:T(1,128)} %reshape.13), calls=%async_computation | async-start | bytes 2097152 | tf_op jit(solution)/shard_map/all_to_all | solution.py:19
  56.8 0.0 reduce-scatter.2.cloned.1.call-start
  56.9 0.0 copy-done.1
  56.9 30.4 %all_gather.3 = f32[256,64]{1,0:T(8,128)S(1)} all-gather(f32[16,64]{1,0:T(8,128)S(1)} %copy-done.1), channel_id=1, replica_groups=mesh['wa'=16,'an'=8] {'wa'}, dimensions={0}, use_global_device_ids=true | all-gather | bytes 69632 | tf_op jit(solution)/shard_map/all_gather | solution.py:20
  87.2 0.0 all-to-all-done
  87.2 0.5 broadcast.1
  87.7 3.3 %reduce = f32[16,16384]{1,0:T(8,128)S(1)} reduce(f32[16,1,16384]{2,1,0:T(1,128)S(1)} %all-to-all-done, f32[]{:T(128)} %broadcast.1), dimensions={1}, to_apply=%all_to_all.26.reduce_sub_computation | reduce | bytes 2097156 | tf_op jit(solution)/shard_map/all_to_all | solution.py:19
  91.0 4.8 %reshape.14 = f32[64,16,16,16]{3,2,1,0:T(8,128)} reshape(f32[16,16384]{1,0:T(8,128)S(1)} %reduce) | data formatting | bytes 2097152
  95.9 9.7 %copy.23 = f32[16,16,16,16,4]{2,1,3,4,0:T(8,128)} copy(f32[16,16,16,16,4]{3,2,0,4,1:T(8,128)} %bitcast.55) | data formatting | bytes 2097152 | tf_op jit(solution)/shard_map/all_to_all | solution.py:19
  105.5 6.1 %all_to_all.29 = f32[16,256,16,4]{1,2,3,0:T(8,128)S(1)} reshape(f32[16,16,16,16,4]{2,1,3,4,0:T(8,128)} %copy.23) | data formatting | bytes 2097152 | tf_op jit(solution)/shard_map/all_to_all | solution.py:19
  111.6 1.0 fusion.7
  112.6 0.3 reshape.15
  113.0 11.2 %all_to_all.36 = f32[8,1,8192]{2,1,0:T(1,128)S(1)} all-to-all(f32[8,1,8192]{2,1,0:T(1,128)S(1)} %reshape.15), channel_id=1, replica_groups=mesh['wa'=16,'an'=8] {'an'}, dimensions={0} | all-to-all | bytes 524288 | tf_op jit(solution)/shard_map/all_to_all | solution.py:22
  124.2 1.3 reduce.1
  125.5 0.2 reshape.16
  125.7 1.2 convolution_bitcast_fusion.1
  126.9 0.0 reduce-scatter.2.cloned.1.call-update
  127.0 29.1 %reduce-scatter.2.cloned.1.call-done = f32[16,128]{1,0:T(8,128)} async-done(((f32[128,128]{1,0:T(8,128)}), f32[16,128]{1,0:T(8,128)}) %reduce-scatter.2.cloned.1.call-update) | async-done | bytes 8208 | tf_op jit(solution)/shard_map/reduce_scatter | solution.py:24
  156.1 39.2 %psum.7 = f32[16,128]{1,0:T(8,128)S(1)} all-reduce(f32[16,128]{1,0:T(8,128)} %reduce-scatter.2.cloned.1.call-done), channel_id=1, replica_groups=mesh['wa'=16,'an'=8] {'wa'}, use_global_device_ids=true, to_apply=%region_1.0 | all-reduce | flops 2048 | bytes 16384 | tf_op jit(solution)/shard_map/psum | solution.py:25
  195.2 0.6 broadcast_multiply_fusion
  (1 shorter events, 0.0 us)
Async XLA Ops:
  6.5 22.6 %copy-start = (f32[256,64]{0,1:T(8,128)S(1)}, f32[256,64]{0,1:T(8,128)}, u32[]{:S(2)}) copy-start(f32[256,64]{0,1:T(8,128)} %param.5) | copy-start | bytes 196612
  40.2 16.6 %copy-start.1 = (f32[16,64]{1,0:T(8,128)S(1)}, f32[16,64]{1,0:T(8,128)}, u32[]{:S(2)}) copy-start(f32[16,64]{1,0:T(8,128)} %param.6) | copy-start | bytes 12292
  47.3 39.9 %all-to-all-start = ((f32[16,1,16384]{2,1,0:T(1,128)}), f32[16,1,16384]{2,1,0:T(1,128)S(1)}, u32[]{:S(2)}, u32[]{:S(2)}) async-start(f32[16,1,16384]{2,1,0:T(1,128)} %reshape.13), calls=%async_computation | async-start | bytes 2097152 | tf_op jit(solution)/shard_map/all_to_all | solution.py:19
  56.8 99.3 %reduce-scatter.2.cloned.1.call-start = ((), (), s32[]{:S(2)}) async-start(), calls=%async_computation.3 | async-start | bytes 73728 | tf_op jit(solution)/shard_map/reduce_scatter | solution.py:24
Sparse Core Ops, SparseCore 0:
  127.1 28.9 reduce-scatter.1

commit v2 on v1

v2 whole, which is shorter than its diff:
```python
import jax
import jax.numpy as jnp
from jax import lax
from jax.sharding import PartitionSpec as P


def on_device(mass_field, factor_one, factor_two, factor_four):
    highest = lax.Precision.HIGHEST
    species_count, fibre_cells, slab_cells, first_cells = mass_field.shape
    rank_one = factor_one.shape[1]
    rank_two = factor_two.shape[1]
    rank_four = factor_four.shape[1]
    fibre_parts = lax.axis_size("wa")
    slab_parts = lax.axis_size("an")
    devices = fibre_parts * slab_parts
    columns = rank_one * rank_four // devices
    cells = fibre_cells * slab_cells
    reduced = jnp.dot(factor_four.T, mass_field.reshape(species_count, -1), precision=highest)
    reduced = reduced.reshape(rank_four, cells, first_cells)
    mixed = jnp.einsum("ir,qci->rqc", factor_one, reduced, precision=highest)
    mixed = mixed.reshape(devices, columns, cells)
    pieces = fibre_cells * rank_two // cells
    own_two = factor_two.reshape(pieces, 1, cells)
    piece = lax.dynamic_index_in_dim(own_two, lax.axis_index("an") % pieces, 0, keepdims=False)
    payload = jnp.concatenate(
        [mixed, jnp.broadcast_to(piece[None], (devices, 1, cells))], axis=1
    )
    payload = lax.all_to_all(payload, ("wa", "an"), 0, 0, tiled=True)
    payload = payload.reshape(fibre_parts, slab_parts, columns + 1, cells)
    whole_two = payload[:, :pieces, columns, :].reshape(fibre_parts * fibre_cells, rank_two)
    gathered = payload[:, :, :columns, :].reshape(
        fibre_parts, slab_parts, columns, fibre_cells, slab_cells
    )
    whole_two = whole_two.reshape(fibre_parts, fibre_cells, rank_two)
    projected = jnp.einsum("wacjk,wjp->akcp", gathered, whole_two, precision=highest)
    projected = projected.reshape(slab_parts * slab_cells, columns * rank_two)
    partial_gram = jnp.dot(projected, projected.T, precision=highest)
    row_blocks = partial_gram.reshape(1, slab_parts, slab_cells, slab_parts * slab_cells)
    row_blocks = jnp.broadcast_to(
        row_blocks, (fibre_parts, slab_parts, slab_cells, slab_parts * slab_cells)
    ).reshape(devices, slab_cells, slab_parts * slab_cells)
    row_blocks = lax.all_to_all(row_blocks, ("wa", "an"), 0, 0, tiled=True)
    gram_rows = jnp.sum(row_blocks, axis=0)
    return gram_rows / (rank_one * rank_two * rank_four)


def solution(mesh):
    in_specs = (P(None, "wa", "an", None), P(), P("wa", None), P())
    out_specs = P("an", None)
    return jax.shard_map(
        on_device, mesh=mesh, in_specs=in_specs, out_specs=out_specs, check_vma=False
    )
```

time: 203 us -> 117 us (0.58)
  waiting for transfers between devices: 29.1 us -> 0 us
  local copies, waits for them, and re-layouts: 36.5 us -> 8.39 us
  blocking collectives: 80.8 us -> 65.2 us
  matrix products: 28.1 us -> 41.7 us
  between operations: 13.5 us -> 0.13 us
  starting transfers between devices: 9.49 us -> 0 us
  other arithmetic: 5.15 us -> 0.91 us
    all_to_all x1 -> x2, blocking collectives: 11.2 us -> 65.2 us  [the longest x1 41.7 us: on_device(): payload = lax.all_to_all(payload, ('wa', 'an'), 0, 0, tiled=True)]
    psum x1 -> x0, blocking collectives: 39.2 us -> none  [on_device(): gram_rows = lax.psum(gram_rows, 'wa')]
    all_gather x1 -> x0, blocking collectives: 30.4 us -> none  [on_device(): whole_two = lax.all_gather(factor_two, 'wa', axis=0, tiled=True)]
    reduce_scatter x1 -> x0, waiting for transfers between devices: 29.1 us -> none  [on_device(): lax.psum_scatter(partial_gram, 'an', scatter_dimension=0, tiled=True)]
    all_to_all x4 -> x1, local copies, waits for them, and re-layouts: 16.3 us -> 0.69 us  [on_device(): payload = lax.all_to_all(payload, ('wa', 'an'), 0, 0, tiled=True)]
    dot_general x3, matrix products: 5.59 us -> 19.2 us  [the longest x1 15.5 us: on_device(): jnp.einsum('wacjk,wjp->akcp', gathered, whole_two, precision=highest)]
    unnamed x8 -> x2, local copies, waits for them, and re-layouts: 12.5 us -> 0.01 us
    all_to_all x1 -> x0, starting transfers between devices: 9.46 us -> none  [on_device(): mixed_rows = lax.all_to_all(mixed_rows, 'wa', 3, 1, tiled=True)]
  transfers between devices with their start and end apart: 2 -> 0, of which waited for: 1 -> 0; matrix products, arithmetic and copies ran while one was open for 0% -> 0% of each run, Pallas kernels for 0% -> 0%
where the time goes in v2:
time: 117 us; the launch traced here: 116 us
  blocking collectives  65.2 us (56%)
  matrix products  41.7 us (36%)
  local copies, waits for them, and re-layouts  8.39 us (7%)
    all_to_all x1, blocking collectives, on_device(): payload = lax.all_to_all(payload, ('wa', 'an'), 0, 0, tiled=True)  41.7 us
    all_to_all x1, blocking collectives, on_device(): row_blocks = lax.all_to_all(row_blocks, ('wa', 'an'), 0, 0, tiled=True)  23.5 us
    dot_general x1, matrix products, on_device(): jnp.dot(factor_four.T, mass_field.reshape(species_count, -1), precision=h...  22.5 us
    dot_general x1, matrix products, on_device(): jnp.einsum('wacjk,wjp->akcp', gathered, whole_two, precision=highest)  15.5 us
    reshape x1, local copies, waits for them, and re-layouts, on_device(): payload[:, :, :columns, :]  4.66 us
    dot_general x1, matrix products, on_device(): mixed = jnp.einsum('ir,qci->rqc', factor_one, reduced, precision=highest)  3.41 us

profile of v2, /device:TPU:1, one launch (start us, length us, event | category | flops | bytes accessed | tf_op | source)
XLA Modules:
  0.0 116.4 jit_solution(876966069621667744)
XLA Ops:
  0.0 0.0 copy-start
  0.0 0.8 reshape.36
  0.8 22.5 %fusion = f32[16,256,256]{2,0,1:T(8,128)S(1)} fusion(f32[64,16]{0,1:T(8,128)} %param.7, f32[8,8,256,256]{3,2,1,0:T(8,128)} %bitcast.47), kind=kOutput, calls=%fused_computation | convolution fusion | flops 805306368 | bytes 20975616 | tf_op jit(solution)/shard_map/dot_general | solution.py:18
  23.3 0.0 copy-done
  23.3 3.4 %convolution_bitcast_fusion = f32[64,16,256]{0,1,2:T(8,128)S(1)} fusion(f32[16,256,256]{2,0,1:T(8,128)S(1)} %fusion, f32[256,64]{0,1:T(8,128)S(1)} %copy-done), kind=kOutput, calls=%fused_computation.6 | convolution fusion | flops 805306368 | bytes 5308416 | tf_op jit(solution)/shard_map/ir,qci->rqc/dot_general | solution.py:20
  26.8 1.4 %copy.17 = f32[64,16,256]{2,1,0:T(8,128)S(1)} copy(f32[64,16,256]{0,1,2:T(8,128)S(1)} %convolution_bitcast_fusion) | data formatting | bytes 2097152 | tf_op jit(solution)/shard_map/ir,qci->rqc/dot_general | solution.py:20
  28.2 0.1 broadcast_in_dim.14
  28.3 0.2 pad_maximum_fusion
  28.5 41.7 %all_to_all.10 = f32[128,9,256]{2,1,0:T(8,128)S(1)} all-to-all(f32[128,9,256]{2,1,0:T(8,128)S(1)} %pad_maximum_fusion), channel_id=1, replica_groups=mesh['wa'=16,'an'=8] {'wa','an'}, dimensions={0} | all-to-all | bytes 2359296 | tf_op jit(solution)/shard_map/all_to_all | solution.py:28
  70.2 0.7 copy.43
  70.9 0.1 slice.9
  71.0 0.1 reshape.44
  71.1 4.7 %reshape.48 = f32[16,8,8,16,16]{4,3,1,0,2:T(8,128)} reshape(f32[16,8,8,256]{3,1,0,2:T(8,128)S(1)} %slice.9) | data formatting | bytes 2097152 | tf_op jit(solution)/shard_map/reshape | solution.py:31
  75.7 15.5 %fusion.5 = f32[8,16,8,64]{3,1,2,0:T(8,128)S(1)} fusion(f32[16,8,8,16,16]{4,3,1,0,2:T(8,128)} %reshape.48, f32[16,16,64,1,1]{2,1,0,3,4:T(8,128)S(1)} %reshape.44), kind=kOutput, calls=%fused_computation.7 | convolution fusion | flops 201326592 | bytes 1376256 | tf_op jit(solution)/shard_map/wacjk,wjp->akcp/dot_general | solution.py:35
  91.2 0.2 copy.21
  91.4 0.1 reshape.46
  91.5 0.1 reshape.39
  91.7 0.4 fusion.11
  92.0 0.1 broadcast_in_dim.15
  92.1 23.5 %all_to_all.11 = f32[128,16,128]{2,1,0:T(8,128)S(1)} all-to-all(f32[128,16,128]{2,1,0:T(8,128)S(1)} %bitcast.51), channel_id=1, replica_groups=mesh['wa'=16,'an'=8] {'wa','an'}, dimensions={0} | all-to-all | bytes 2097152 | tf_op jit(solution)/shard_map/all_to_all | solution.py:42
  115.7 0.1 reduce_sum.9
  115.8 0.6 broadcast_multiply_fusion
  (2 shorter events, 0.0 us)
Async XLA Ops:
  0.0 23.3 %copy-start = (f32[256,64]{0,1:T(8,128)S(1)}, f32[256,64]{0,1:T(8,128)}, u32[]{:S(2)}) copy-start(f32[256,64]{0,1:T(8,128)} %param.5) | copy-start | bytes 196612

commit v3 on v2

v3 whole, which is shorter than its diff:
```python
import jax
import jax.numpy as jnp
from jax import lax
from jax.sharding import PartitionSpec as P


def on_device(mass_field, factor_one, factor_two, factor_four):
    highest = lax.Precision.HIGHEST
    species_count, fibre_cells, slab_cells, first_cells = mass_field.shape
    rank_one = factor_one.shape[1]
    rank_two = factor_two.shape[1]
    rank_four = factor_four.shape[1]
    fibre_parts = lax.axis_size("wa")
    slab_parts = lax.axis_size("an")
    devices = fibre_parts * slab_parts
    columns = rank_one * rank_four // devices
    halves = rank_four // columns
    spread = jnp.dot(
        mass_field.reshape(species_count * fibre_cells * slab_cells, first_cells),
        factor_one,
        precision=highest,
    ).reshape(species_count, fibre_cells, slab_cells, rank_one)
    mixed = jnp.einsum(
        "shc,sjkr->rhjkc",
        factor_four.reshape(species_count, halves, columns),
        spread,
        precision=highest,
    )
    block = fibre_cells * slab_cells * columns
    mixed = mixed.reshape(devices, block)
    piece_len = fibre_cells * rank_two // slab_parts
    own_two = factor_two.reshape(slab_parts, piece_len)
    piece = lax.dynamic_index_in_dim(own_two, lax.axis_index("an"), 0, keepdims=True)
    payload = jnp.concatenate([mixed, jnp.broadcast_to(piece, (devices, piece_len))], axis=1)
    payload = lax.all_to_all(payload, ("wa", "an"), 0, 0, tiled=True)
    whole_two = payload[:, block:].reshape(fibre_parts, fibre_cells, rank_two)
    gathered = payload[:, :block].reshape(fibre_parts, slab_parts, fibre_cells, slab_cells * columns)
    projected = jnp.einsum("wajx,wjp->axp", gathered, whole_two, precision=highest)
    projected = projected.reshape(slab_parts * slab_cells, columns * rank_two)
    partial_gram = jnp.dot(projected, projected.T, precision=highest)
    row_blocks = partial_gram.reshape(1, slab_parts, slab_cells, slab_parts * slab_cells)
    row_blocks = jnp.broadcast_to(
        row_blocks, (fibre_parts, slab_parts, slab_cells, slab_parts * slab_cells)
    ).reshape(devices, slab_cells, slab_parts * slab_cells)
    row_blocks = lax.all_to_all(row_blocks, ("wa", "an"), 0, 0, tiled=True)
    gram_rows = jnp.sum(row_blocks, axis=0)
    return gram_rows / (rank_one * rank_two * rank_four)


def solution(mesh):
    in_specs = (P(None, "wa", "an", None), P(), P("wa", None), P())
    out_specs = P("an", None)
    return jax.shard_map(
        on_device, mesh=mesh, in_specs=in_specs, out_specs=out_specs, check_vma=False
    )
```

time: 117 us -> 120 us (1.026)
  local copies, waits for them, and re-layouts: 8.39 us -> 29 us
  blocking collectives: 65.2 us -> 54.6 us
  matrix products: 41.7 us -> 35.3 us
    transpose x1, local copies, waits for them, and re-layouts: 0.16 us -> 13.7 us  [on_device(): jnp.einsum('shc,sjkr->rhjkc', factor_four.reshape(species_count, halves,...]
    all_to_all x1, blocking collectives: 41.7 us -> 31.4 us  [on_device(): payload = lax.all_to_all(payload, ('wa', 'an'), 0, 0, tiled=True)]
    reshape x2 -> x3, local copies, waits for them, and re-layouts: 5.46 us -> 12.8 us  [the longest x1 12.6 us: on_device(): mixed = mixed.reshape(devices, block)]
    dot_general x3, matrix products: 41.4 us -> 34.9 us  [the longest x1 28.7 us: on_device(): jnp.dot(mass_field.reshape(species_count * fibre_cells * slab_cells, firs...]
    dot_general x1 -> x0, local copies, waits for them, and re-layouts: 1.44 us -> none  [on_device(): mixed = jnp.einsum('ir,qci->rqc', factor_one, reduced, precision=highest)]
where the time goes in v3:
time: 120 us
  blocking collectives  54.6 us (46%)
  matrix products  35.3 us (29%)
  local copies, waits for them, and re-layouts  29 us (24%)
    all_to_all x1, blocking collectives, on_device(): payload = lax.all_to_all(payload, ('wa', 'an'), 0, 0, tiled=True)  31.4 us
    dot_general x1, matrix products, on_device(): jnp.dot(mass_field.reshape(species_count * fibre_cells * slab_cells, firs...  28.7 us
    all_to_all x1, blocking collectives, on_device(): row_blocks = lax.all_to_all(row_blocks, ('wa', 'an'), 0, 0, tiled=True)  23.2 us
    transpose x1, local copies, waits for them, and re-layouts, on_device(): jnp.einsum('shc,sjkr->rhjkc', factor_four.reshape(species_count, halves,...  13.7 us
    reshape x1, local copies, waits for them, and re-layouts, on_device(): mixed = mixed.reshape(devices, block)  12.6 us
    dot_general x1, matrix products, on_device(): jnp.einsum('shc,sjkr->rhjkc', factor_four.reshape(species_count, halves,...  4.41 us

profile of v3, /device:TPU:1, one launch (start us, length us, event | category | flops | bytes accessed | tf_op | source)
XLA Modules:
  0.0 119.8 jit_solution(11587582678164971819)
XLA Ops:
  0.0 0.0 copy-start
  0.0 0.8 copy-done
  0.8 0.0 copy-start.2
  0.8 28.7 %fusion = f32[64,16,16,64]{3,0,2,1:T(8,128)S(1)} fusion(f32[64,16,16,256]{3,2,1,0:T(8,128)} %param.4, f32[256,64]{0,1:T(8,128)S(1)} %copy-done), kind=kOutput, calls=%fused_computation | convolution fusion | flops 3221225472 | bytes 21037056 | tf_op jit(solution)/shard_map/dot_general | solution.py:18
  29.5 0.0 copy-done.2
  29.6 4.4 %fusion.4 = f32[64,2,16,16,8]{0,4,1,3,2:T(8,128)S(1)} fusion(f32[64,16,16,64]{3,0,2,1:T(8,128)S(1)} %fusion, f32[64,16]{0,1:T(8,128)S(1)} %copy-done.2), kind=kOutput, calls=%fused_computation.4 | convolution fusion | flops 201326592 | bytes 5246976 | tf_op jit(solution)/shard_map/shc,sjkr->rhjkc/dot_general | solution.py:23
  34.0 13.7 %copy.16 = f32[64,2,16,16,8]{4,3,2,1,0:T(8,128)} copy(f32[64,2,16,16,8]{0,4,1,3,2:T(8,128)S(1)} %fusion.4) | data formatting | bytes 2097152 | tf_op jit(solution)/shard_map/shc,sjkr->rhjkc/transpose | solution.py:23
  47.7 0.0 copy-start.1
  47.7 12.6 %reshape.37 = f32[128,2048]{1,0:T(8,128)S(1)} reshape(f32[64,2,16,16,8]{4,3,2,1,0:T(8,128)} %copy.16) | data formatting | bytes 2097152 | tf_op jit(solution)/shard_map/reshape | solution.py:30
  60.3 0.0 copy-done.1
  60.3 0.1 reshape.38
  60.4 0.1 maximum_bitcast_fusion
  60.5 1.1 copy.17
  61.6 31.4 %all_to_all.17 = f32[128,1,2176]{2,1,0:T(1,128)S(1)} all-to-all(f32[128,1,2176]{2,1,0:T(1,128)S(1)} %copy.17), channel_id=1, replica_groups=mesh['wa'=16,'an'=8] {'wa','an'}, dimensions={0} | all-to-all | bytes 2228224 | tf_op jit(solution)/shard_map/all_to_all | solution.py:35
  93.0 0.1 copy.36
  93.1 0.1 slice_bitcast_fusion
  93.2 0.1 reshape.47
  93.3 1.8 %convolution_bitcast_fusion = f32[8,128,64]{2,1,0:T(8,128)S(1)} fusion(f32[16,8,16,128]{3,1,2,0:T(8,128)S(1)} %slice_bitcast_fusion, f32[16,16,64,1]{2,1,0,3:T(8,128)S(1)} %reshape.47), kind=kOutput, calls=%fused_computation.5 | convolution fusion | flops 201326592 | bytes 1376256 | tf_op jit(solution)/shard_map/wajx,wjp->axp/dot_general | solution.py:38
  95.1 0.1 reshape.41
  95.3 0.1 reshape.49
  95.4 0.4 fusion.12
  95.8 0.1 broadcast_in_dim.14
  95.9 23.2 %all_to_all.18 = f32[128,16,128]{2,1,0:T(8,128)S(1)} all-to-all(f32[128,16,128]{2,1,0:T(8,128)S(1)} %bitcast.48), channel_id=1, replica_groups=mesh['wa'=16,'an'=8] {'wa','an'}, dimensions={0} | all-to-all | bytes 2097152 | tf_op jit(solution)/shard_map/all_to_all | solution.py:45
  119.1 0.1 reduce_sum.9
  119.2 0.6 broadcast_multiply_fusion
  (3 shorter events, 0.0 us)
Async XLA Ops:
  0.0 0.8 copy-start
  0.8 28.7 %copy-start.2 = (f32[64,16]{0,1:T(8,128)S(1)}, f32[64,16]{0,1:T(8,128)}, u32[]{:S(2)}) copy-start(f32[64,16]{0,1:T(8,128)} %param.7) | copy-start | bytes 12292
  47.7 12.6 %copy-start.1 = (f32[16,64]{1,0:T(8,128)S(1)}, f32[16,64]{1,0:T(8,128)}, u32[]{:S(2)}) copy-start(f32[16,64]{1,0:T(8,128)} %param.6) | copy-start | bytes 12292

commit v4 on v3

--- a/solution.py
+++ b/solution.py
@@ -15,15 +15,16 @@
     devices = fibre_parts * slab_parts
     columns = rank_one * rank_four // devices
     halves = rank_four // columns
-    spread = jnp.dot(
-        mass_field.reshape(species_count * fibre_cells * slab_cells, first_cells),
+    reduced = jnp.einsum(
+        "shc,sjki->hjkci",
+        factor_four.reshape(species_count, halves, columns),
+        mass_field,
+        precision=highest,
+    )
+    mixed = lax.dot_general(
         factor_one,
-        precision=highest,
-    ).reshape(species_count, fibre_cells, slab_cells, rank_one)
-    mixed = jnp.einsum(
-        "shc,sjkr->rhjkc",
-        factor_four.reshape(species_count, halves, columns),
-        spread,
+        reduced.reshape(-1, first_cells),
+        (((0,), (1,)), ((), ())),
         precision=highest,
     )
     block = fibre_cells * slab_cells * columns

time: 120 us -> 86.6 us (0.72)
  local copies, waits for them, and re-layouts: 29 us -> 2.21 us
  matrix products: 35.3 us -> 28.7 us
    transpose x1, local copies, waits for them, and re-layouts: 13.7 us -> 0.57 us  [on_device(): jnp.einsum('shc,sjki->hjkci', factor_four.reshape(species_count, halves,...]
    reshape x1, local copies, waits for them, and re-layouts: 12.6 us -> 0.16 us  [on_device(): mixed = mixed.reshape(devices, block)]
    dot_general x2, matrix products: 33.1 us -> 26.5 us  [the longest x1 22.3 us: on_device(): jnp.einsum('shc,sjki->hjkci', factor_four.reshape(species_count, halves,...]
where the time goes in v4:
time: 86.6 us; the launch traced here: 86.4 us
  blocking collectives  54.6 us (63%)
  matrix products  28.7 us (33%)
  local copies, waits for them, and re-layouts  2.21 us (3%)
    all_to_all x1, blocking collectives, on_device(): payload = lax.all_to_all(payload, ('wa', 'an'), 0, 0, tiled=True)  31.4 us
    all_to_all x1, blocking collectives, on_device(): row_blocks = lax.all_to_all(row_blocks, ('wa', 'an'), 0, 0, tiled=True)  23.2 us
    dot_general x1, matrix products, on_device(): jnp.einsum('shc,sjki->hjkci', factor_four.reshape(species_count, halves,...  22.3 us
    dot_general x1, matrix products, on_device(): lax.dot_general(factor_one, reduced.reshape(-1, first_cells), (((0,), (1,...  4.19 us
    dot_general x1, matrix products, on_device(): jnp.einsum('wajx,wjp->axp', gathered, whole_two, precision=highest)  1.81 us

profile of v4, /device:TPU:1, one launch (start us, length us, event | category | flops | bytes accessed | tf_op | source)
XLA Modules:
  0.0 86.4 jit_solution(12650158898500209718)
XLA Ops:
  0.0 0.0 copy-start
  0.0 22.3 %fusion.2 = f32[2,16,16,8,256]{4,3,0,2,1:T(8,128)S(1)} fusion(f32[64,16,16,256,1]{3,2,1,0,4:T(8,128)} %bitcast.36, f32[64,16]{0,1:T(8,128)} %param.7), kind=kOutput, calls=%fused_computation.3 | convolution fusion | flops 805306368 | bytes 20975616 | tf_op jit(solution)/shard_map/shc,sjki->hjkci/dot_general | solution.py:18
  22.3 0.6 copy.17
  22.9 0.0 copy-start.1
  22.9 0.0 copy-done
  22.9 4.2 %convolution_bitcast_fusion = f32[64,4096]{1,0:T(8,128)S(1)} fusion(f32[4096,256]{1,0:T(8,128)S(1)} %bitcast.37, f32[256,64]{0,1:T(8,128)S(1)} %copy-done), kind=kOutput, calls=%fused_computation.2 | convolution fusion | flops 805306368 | bytes 5308416 | tf_op jit(solution)/shard_map/dot_general | solution.py:24
  27.1 0.2 reshape.37
  27.3 0.0 copy-done.1
  27.3 0.1 reshape.38
  27.4 0.1 pad_maximum_fusion
  27.4 0.8 all_to_all.11
  28.2 31.4 %all_to_all.17 = f32[128,1,2176]{2,1,0:T(1,128)S(1)} all-to-all(f32[128,1,2176]{2,1,0:T(1,128)S(1)} %all_to_all.11), channel_id=1, replica_groups=mesh['wa'=16,'an'=8] {'wa','an'}, dimensions={0} | all-to-all | bytes 2228224 | tf_op jit(solution)/shard_map/all_to_all | solution.py:36
  59.6 0.1 copy.39
  59.7 0.1 slice_bitcast_fusion
  59.8 0.1 reshape.46
  59.9 1.8 %convolution_bitcast_fusion.1 = f32[8,128,64]{2,1,0:T(8,128)S(1)} fusion(f32[16,8,16,128]{3,1,2,0:T(8,128)S(1)} %slice_bitcast_fusion, f32[16,16,64,1]{2,1,0,3:T(8,128)S(1)} %reshape.46), kind=kOutput, calls=%fused_computation.4 | convolution fusion | flops 201326592 | bytes 1376256 | tf_op jit(solution)/shard_map/wajx,wjp->axp/dot_general | solution.py:39
  61.7 0.1 reshape.41
  61.9 0.1 reshape.48
  62.0 0.4 fusion.9
  62.4 0.1 broadcast_in_dim.14
  62.5 23.2 %all_to_all.18 = f32[128,16,128]{2,1,0:T(8,128)S(1)} all-to-all(f32[128,16,128]{2,1,0:T(8,128)S(1)} %bitcast.40), channel_id=1, replica_groups=mesh['wa'=16,'an'=8] {'wa','an'}, dimensions={0} | all-to-all | bytes 2097152 | tf_op jit(solution)/shard_map/all_to_all | solution.py:46
  85.7 0.1 reduce_sum.9
  85.8 0.6 broadcast_multiply_fusion
  (3 shorter events, 0.0 us)
Async XLA Ops:
  0.0 22.9 %copy-start = (f32[256,64]{0,1:T(8,128)S(1)}, f32[256,64]{0,1:T(8,128)}, u32[]{:S(2)}) copy-start(f32[256,64]{0,1:T(8,128)} %param.5) | copy-start | bytes 196612
  22.9 4.4 %copy-start.1 = (f32[16,64]{1,0:T(8,128)S(1)}, f32[16,64]{1,0:T(8,128)}, u32[]{:S(2)}) copy-start(f32[16,64]{1,0:T(8,128)} %param.6) | copy-start | bytes 12292

commit v5 on v4

--- a/solution.py
+++ b/solution.py
@@ -19,7 +19,7 @@
         "shc,sjki->hjkci",
         factor_four.reshape(species_count, halves, columns),
         mass_field,
-        precision=highest,
+        precision=lax.Precision.HIGH,
     )
     mixed = lax.dot_general(
         factor_one,

time: 86.6 us -> 83.3 us (0.962)
  matrix products: 28.7 us -> 25.5 us
    dot_general x1, matrix products: 22.3 us -> 19.1 us  [on_device(): jnp.einsum('shc,sjki->hjkci', factor_four.reshape(species_count, halves,...]
where the time goes in v5:
time: 83.3 us; the launch traced here: 83.2 us
  blocking collectives  54.6 us (66%)
  matrix products  25.5 us (31%)
  local copies, waits for them, and re-layouts  2.21 us (3%)
    all_to_all x1, blocking collectives, on_device(): payload = lax.all_to_all(payload, ('wa', 'an'), 0, 0, tiled=True)  31.4 us
    all_to_all x1, blocking collectives, on_device(): row_blocks = lax.all_to_all(row_blocks, ('wa', 'an'), 0, 0, tiled=True)  23.2 us
    dot_general x1, matrix products, on_device(): jnp.einsum('shc,sjki->hjkci', factor_four.reshape(species_count, halves,...  19.1 us
    dot_general x1, matrix products, on_device(): lax.dot_general(factor_one, reduced.reshape(-1, first_cells), (((0,), (1,...  4.18 us
    dot_general x1, matrix products, on_device(): jnp.einsum('wajx,wjp->axp', gathered, whole_two, precision=highest)  1.81 us

profile of v5, /device:TPU:1, one launch (start us, length us, event | category | flops | bytes accessed | tf_op | source)
XLA Modules:
  0.0 83.2 jit_solution(14436615943888771562)
XLA Ops:
  0.0 0.0 copy-start
  0.0 19.1 %fusion.2 = f32[2,16,16,8,256]{4,3,0,2,1:T(8,128)S(1)} fusion(f32[64,16,16,256,1]{3,2,1,0,4:T(8,128)} %bitcast.36, f32[64,16]{0,1:T(8,128)} %param.7), kind=kOutput, calls=%fused_computation.3 | convolution fusion | flops 402653184 | bytes 20975616 | tf_op jit(solution)/shard_map/shc,sjki->hjkci/dot_general | solution.py:18
  19.1 0.6 copy.17
  19.7 0.0 copy-start.1
  19.7 0.0 copy-done
  19.7 4.2 %convolution_bitcast_fusion = f32[64,4096]{1,0:T(8,128)S(1)} fusion(f32[4096,256]{1,0:T(8,128)S(1)} %bitcast.37, f32[256,64]{0,1:T(8,128)S(1)} %copy-done), kind=kOutput, calls=%fused_computation.2 | convolution fusion | flops 805306368 | bytes 5308416 | tf_op jit(solution)/shard_map/dot_general | solution.py:24
  23.9 0.2 reshape.37
  24.1 0.0 copy-done.1
  24.1 0.1 reshape.38
  24.1 0.1 pad_maximum_fusion
  24.2 0.8 all_to_all.11
  25.0 31.4 %all_to_all.17 = f32[128,1,2176]{2,1,0:T(1,128)S(1)} all-to-all(f32[128,1,2176]{2,1,0:T(1,128)S(1)} %all_to_all.11), channel_id=1, replica_groups=mesh['wa'=16,'an'=8] {'wa','an'}, dimensions={0} | all-to-all | bytes 2228224 | tf_op jit(solution)/shard_map/all_to_all | solution.py:36
  56.4 0.1 copy.39
  56.5 0.1 slice_bitcast_fusion
  56.6 0.1 reshape.46
  56.7 1.8 %convolution_bitcast_fusion.1 = f32[8,128,64]{2,1,0:T(8,128)S(1)} fusion(f32[16,8,16,128]{3,1,2,0:T(8,128)S(1)} %slice_bitcast_fusion, f32[16,16,64,1]{2,1,0,3:T(8,128)S(1)} %reshape.46), kind=kOutput, calls=%fused_computation.4 | convolution fusion | flops 201326592 | bytes 1376256 | tf_op jit(solution)/shard_map/wajx,wjp->axp/dot_general | solution.py:39
  58.5 0.1 reshape.41
  58.7 0.1 reshape.48
  58.8 0.4 fusion.9
  59.2 0.1 broadcast_in_dim.14
  59.3 23.2 %all_to_all.18 = f32[128,16,128]{2,1,0:T(8,128)S(1)} all-to-all(f32[128,16,128]{2,1,0:T(8,128)S(1)} %bitcast.40), channel_id=1, replica_groups=mesh['wa'=16,'an'=8] {'wa','an'}, dimensions={0} | all-to-all | bytes 2097152 | tf_op jit(solution)/shard_map/all_to_all | solution.py:46
  82.5 0.1 reduce_sum.9
  82.6 0.6 broadcast_multiply_fusion
  (3 shorter events, 0.0 us)
Async XLA Ops:
  0.0 19.7 %copy-start = (f32[256,64]{0,1:T(8,128)S(1)}, f32[256,64]{0,1:T(8,128)}, u32[]{:S(2)}) copy-start(f32[256,64]{0,1:T(8,128)} %param.5) | copy-start | bytes 196612
  19.7 4.4 %copy-start.1 = (f32[16,64]{1,0:T(8,128)S(1)}, f32[16,64]{1,0:T(8,128)}, u32[]{:S(2)}) copy-start(f32[16,64]{1,0:T(8,128)} %param.6) | copy-start | bytes 12292

commit v6 on v4

--- a/solution.py
+++ b/solution.py
@@ -39,12 +39,12 @@
     projected = jnp.einsum("wajx,wjp->axp", gathered, whole_two, precision=highest)
     projected = projected.reshape(slab_parts * slab_cells, columns * rank_two)
     partial_gram = jnp.dot(projected, projected.T, precision=highest)
-    row_blocks = partial_gram.reshape(1, slab_parts, slab_cells, slab_parts * slab_cells)
-    row_blocks = jnp.broadcast_to(
-        row_blocks, (fibre_parts, slab_parts, slab_cells, slab_parts * slab_cells)
-    ).reshape(devices, slab_cells, slab_parts * slab_cells)
-    row_blocks = lax.all_to_all(row_blocks, ("wa", "an"), 0, 0, tiled=True)
+    row_blocks = partial_gram.reshape(slab_parts, slab_cells, slab_parts * slab_cells)
+    row_blocks = lax.all_to_all(row_blocks, "an", 0, 0, tiled=True)
     gram_rows = jnp.sum(row_blocks, axis=0)
+    gram_rows = jnp.broadcast_to(gram_rows[None], (fibre_parts,) + gram_rows.shape)
+    gram_rows = lax.all_to_all(gram_rows, "wa", 0, 0, tiled=True)
+    gram_rows = jnp.sum(gram_rows, axis=0)
     return gram_rows / (rank_one * rank_two * rank_four)
 
 

time: 86.6 us -> 83.5 us (0.964)
  blocking collectives: 54.6 us -> 51.7 us
    all_to_all x1 -> x2, blocking collectives: 23.2 us -> 20.3 us  [the longest x1 12.7 us: on_device(): gram_rows = lax.all_to_all(gram_rows, 'wa', 0, 0, tiled=True)]
where the time goes in v6:
time: 83.5 us; the launch traced here: 83.3 us
  blocking collectives  51.7 us (62%)
  matrix products  28.7 us (34%)
  local copies, waits for them, and re-layouts  2.13 us (3%)
    all_to_all x1, blocking collectives, on_device(): payload = lax.all_to_all(payload, ('wa', 'an'), 0, 0, tiled=True)  31.4 us
    dot_general x1, matrix products, on_device(): jnp.einsum('shc,sjki->hjkci', factor_four.reshape(species_count, halves,...  22.3 us
    all_to_all x1, blocking collectives, on_device(): gram_rows = lax.all_to_all(gram_rows, 'wa', 0, 0, tiled=True)  12.7 us
    all_to_all x1, blocking collectives, on_device(): row_blocks = lax.all_to_all(row_blocks, 'an', 0, 0, tiled=True)  7.58 us
    dot_general x1, matrix products, on_device(): lax.dot_general(factor_one, reduced.reshape(-1, first_cells), (((0,), (1,...  4.19 us
    dot_general x1, matrix products, on_device(): jnp.einsum('wajx,wjp->axp', gathered, whole_two, precision=highest)  1.81 us

profile of v6, /device:TPU:1, one launch (start us, length us, event | category | flops | bytes accessed | tf_op | source)
XLA Modules:
  0.0 83.3 jit_solution(17115042392701382330)
XLA Ops:
  0.0 0.0 copy-start
  0.0 22.3 %fusion.2 = f32[2,16,16,8,256]{4,3,0,2,1:T(8,128)S(1)} fusion(f32[64,16,16,256,1]{3,2,1,0,4:T(8,128)} %bitcast.35, f32[64,16]{0,1:T(8,128)} %param.7), kind=kOutput, calls=%fused_computation.3 | convolution fusion | flops 805306368 | bytes 20975616 | tf_op jit(solution)/shard_map/shc,sjki->hjkci/dot_general | solution.py:18
  22.3 0.6 copy.17
  22.9 0.0 copy-start.1
  22.9 0.0 copy-done
  22.9 4.2 %convolution_bitcast_fusion = f32[64,4096]{1,0:T(8,128)S(1)} fusion(f32[4096,256]{1,0:T(8,128)S(1)} %bitcast.36, f32[256,64]{0,1:T(8,128)S(1)} %copy-done), kind=kOutput, calls=%fused_computation.2 | convolution fusion | flops 805306368 | bytes 5308416 | tf_op jit(solution)/shard_map/dot_general | solution.py:24
  27.1 0.2 reshape.29
  27.3 0.0 copy-done.1
  27.3 0.1 reshape.30
  27.4 0.1 pad_maximum_fusion
  27.4 0.8 all_to_all.14
  28.2 31.4 %all_to_all.22 = f32[128,1,2176]{2,1,0:T(1,128)S(1)} all-to-all(f32[128,1,2176]{2,1,0:T(1,128)S(1)} %all_to_all.14), channel_id=1, replica_groups=mesh['wa'=16,'an'=8] {'wa','an'}, dimensions={0} | all-to-all | bytes 2228224 | tf_op jit(solution)/shard_map/all_to_all | solution.py:36
  59.6 0.1 copy.39
  59.7 0.1 slice_bitcast_fusion
  59.8 0.1 reshape.36
  59.9 1.8 %convolution_bitcast_fusion.1 = f32[8,128,64]{2,1,0:T(8,128)S(1)} fusion(f32[16,8,16,128]{3,1,2,0:T(8,128)S(1)} %slice_bitcast_fusion, f32[16,16,64,1]{2,1,0,3:T(8,128)S(1)} %reshape.36), kind=kOutput, calls=%fused_computation.4 | convolution fusion | flops 201326592 | bytes 1376256 | tf_op jit(solution)/shard_map/wajx,wjp->axp/dot_general | solution.py:39
  61.7 0.1 dot_general.20
  61.9 0.1 reshape.38
  62.0 0.4 fusion.9
  62.4 7.6 %all_to_all.23 = f32[8,16,128]{2,1,0:T(8,128)S(1)} all-to-all(f32[8,16,128]{2,1,0:T(8,128)S(1)} %fusion.9), channel_id=1, replica_groups=mesh['wa'=16,'an'=8] {'an'}, dimensions={0} | all-to-all | bytes 131072 | tf_op jit(solution)/shard_map/all_to_all | solution.py:43
  70.0 12.7 %all_to_all.24 = f32[16,16,128]{2,1,0:T(8,128)S(1)} all-to-all(f32[16,16,128]{2,1,0:T(8,128)S(1)} %broadcast_in_dim.15), channel_id=1, replica_groups=mesh['wa'=16,'an'=8] {'wa'}, dimensions={0} | all-to-all | bytes 262144 | tf_op jit(solution)/shard_map/all_to_all | solution.py:46
  82.7 0.6 broadcast_multiply_fusion
  (6 shorter events, 0.1 us)
Async XLA Ops:
  0.0 22.9 %copy-start = (f32[256,64]{0,1:T(8,128)S(1)}, f32[256,64]{0,1:T(8,128)}, u32[]{:S(2)}) copy-start(f32[256,64]{0,1:T(8,128)} %param.5) | copy-start | bytes 196612
  22.9 4.4 %copy-start.1 = (f32[16,64]{1,0:T(8,128)S(1)}, f32[16,64]{1,0:T(8,128)}, u32[]{:S(2)}) copy-start(f32[16,64]{1,0:T(8,128)} %param.6) | copy-start | bytes 12292

commit v7 on v6

v7 whole, which is shorter than its diff:
```python
import jax
import jax.numpy as jnp
from jax import lax
from jax.sharding import PartitionSpec as P


def on_device(mass_field, factor_one, factor_two, factor_four):
    highest = lax.Precision.HIGHEST
    species_count, fibre_cells, slab_cells, first_cells = mass_field.shape
    rank_one = factor_one.shape[1]
    rank_two = factor_two.shape[1]
    rank_four = factor_four.shape[1]
    fibre_parts = lax.axis_size("wa")
    slab_parts = lax.axis_size("an")
    devices = fibre_parts * slab_parts
    columns = rank_one * rank_four // devices
    halves = rank_four // columns
    steps = 2
    step_cells = fibre_cells // steps
    block = step_cells * slab_cells * columns
    four = factor_four.reshape(species_count, halves, columns)
    by_fibre = jnp.transpose(mass_field, (1, 2, 0, 3))
    projected = None
    for step in range(steps):
        part = by_fibre[step * step_cells:(step + 1) * step_cells]
        reduced = jnp.einsum("shc,jksi->hjkci", four, part, precision=highest)
        mixed = lax.dot_general(
            factor_one, reduced.reshape(-1, first_cells), (((0,), (1,)), ((), ())), precision=highest
        )
        mixed = mixed.reshape(devices, block)
        piece_len = step_cells * rank_two // slab_parts
        own_two = factor_two[step * step_cells:(step + 1) * step_cells].reshape(slab_parts, piece_len)
        piece = lax.dynamic_index_in_dim(own_two, lax.axis_index("an"), 0, keepdims=True)
        payload = jnp.concatenate([mixed, jnp.broadcast_to(piece, (devices, piece_len))], axis=1)
        payload = lax.all_to_all(payload, ("wa", "an"), 0, 0, tiled=True)
        some_two = payload[:, block:].reshape(fibre_parts, step_cells, rank_two)
        gathered = payload[:, :block].reshape(fibre_parts, slab_parts, step_cells, slab_cells * columns)
        term = jnp.einsum("wajx,wjp->axp", gathered, some_two, precision=highest)
        projected = term if projected is None else projected + term
    projected = projected.reshape(slab_parts * slab_cells, columns * rank_two)
    partial_gram = jnp.dot(projected, projected.T, precision=highest)
    row_blocks = partial_gram.reshape(slab_parts, slab_cells, slab_parts * slab_cells)
    row_blocks = lax.all_to_all(row_blocks, "an", 0, 0, tiled=True)
    gram_rows = jnp.sum(row_blocks, axis=0)
    gram_rows = jnp.broadcast_to(gram_rows[None], (fibre_parts,) + gram_rows.shape)
    gram_rows = lax.all_to_all(gram_rows, "wa", 0, 0, tiled=True)
    gram_rows = jnp.sum(gram_rows, axis=0)
    return gram_rows / (rank_one * rank_two * rank_four)


def solution(mesh):
    in_specs = (P(None, "wa", "an", None), P(), P("wa", None), P())
    out_specs = P("an", None)
    return jax.shard_map(
        on_device, mesh=mesh, in_specs=in_specs, out_specs=out_specs, check_vma=False
    )
```

time: 83.5 us -> 97.4 us (1.17)
  blocking collectives: 51.7 us -> 20.3 us
  local copies, waits for them, and re-layouts: 2.13 us -> 23.7 us
  starting transfers between devices: 0 us -> 17.8 us
  waiting for transfers between devices: 0 us -> 17.1 us
  matrix products: 28.7 us -> 16.9 us
    all_to_all x1 -> x0, blocking collectives: 31.4 us -> none  [on_device(): payload = lax.all_to_all(payload, ('wa', 'an'), 0, 0, tiled=True)]
    all_to_all x0 -> x2, starting transfers between devices: none -> 17.8 us  [on_device(): payload = lax.all_to_all(payload, ('wa', 'an'), 0, 0, tiled=True)]
    all_to_all x0 -> x2, waiting for transfers between devices: none -> 17.1 us  [on_device(): payload = lax.all_to_all(payload, ('wa', 'an'), 0, 0, tiled=True)]
    unnamed x6 -> x9, local copies, waits for them, and re-layouts: 0.18 us -> 16.6 us
    dot_general x2 -> x4, matrix products: 24.1 us -> 12.2 us  [the longest x2 11.2 us: on_device(): reduced = jnp.einsum('shc,jksi->hjkci', four, part, precision=highest)]
    all_to_all x1 -> x4, local copies, waits for them, and re-layouts: 0.77 us -> 4.91 us  [on_device(): payload = lax.all_to_all(payload, ('wa', 'an'), 0, 0, tiled=True)]
    dot_general x1 -> x2, matrix products: 4.19 us -> 4.31 us  [on_device(): lax.dot_general(factor_one, reduced.reshape(-1, first_cells), (((0,), (1,...]
  transfers between devices with their start and end apart: 0 -> 2, of which waited for: 0 -> 2; matrix products, arithmetic and copies ran while one was open for 0% -> 13% of each run, Pallas kernels for 0% -> 0%
where the time goes in v7:
time: 97.4 us; the launch traced here: 97.1 us
  local copies, waits for them, and re-layouts  23.7 us (24%)
  blocking collectives  20.3 us (21%)
  starting transfers between devices  17.8 us (18%)
  waiting for transfers between devices  17.1 us (18%)
  matrix products  16.9 us (17%)
  other arithmetic  1.04 us (1%)
    all_to_all x2, starting transfers between devices, on_device(): payload = lax.all_to_all(payload, ('wa', 'an'), 0, 0, tiled=True)  17.8 us
    all_to_all x2, waiting for transfers between devices, on_device(): payload = lax.all_to_all(payload, ('wa', 'an'), 0, 0, tiled=True)  17.1 us
    unnamed x9, local copies, waits for them, and re-layouts  16.6 us
    all_to_all x1, blocking collectives, on_device(): gram_rows = lax.all_to_all(gram_rows, 'wa', 0, 0, tiled=True)  12.7 us
    dot_general x2, matrix products, on_device(): reduced = jnp.einsum('shc,jksi->hjkci', four, part, precision=highest)  11.2 us
    all_to_all x1, blocking collectives, on_device(): row_blocks = lax.all_to_all(row_blocks, 'an', 0, 0, tiled=True)  7.58 us
    all_to_all x4, local copies, waits for them, and re-layouts, on_device(): payload = lax.all_to_all(payload, ('wa', 'an'), 0, 0, tiled=True)  4.91 us
    dot_general x2, matrix products, on_device(): lax.dot_general(factor_one, reduced.reshape(-1, first_cells), (((0,), (1,...  4.31 us
  transfers between devices with their start and end apart: 2, of which 2 were waited for; matrix products, arithmetic and copies ran while one was open for 13% of the time, Pallas kernels for 0%

profile of v7, /device:TPU:1, one launch (start us, length us, event | category | flops | bytes accessed | tf_op | source)
XLA Modules:
  0.0 97.1 jit_solution(5749833436711791130)
XLA Ops:
  0.0 0.0 copy-start
  0.0 0.0 copy-start.2
  0.0 15.5 %copy.66 = f32[64,16,16,256]{3,0,2,1:T(8,128)S(1)} copy(f32[64,16,16,256]{3,2,1,0:T(8,128)} %param.4) | data formatting | bytes 33554432 | tf_op args[0]
  15.6 0.0 copy-start.1
  15.6 0.0 copy-done.2
  15.6 4.4 %fusion.3 = f32[2,8,16,8,256]{4,3,0,2,1:T(8,128)S(1)} fusion(f32[16,16,64,256]{3,2,1,0:T(8,128)S(1)} %bitcast.82, f32[64,16]{0,1:T(8,128)S(1)} %copy-done.2), kind=kOutput, calls=%fused_computation.8 | convolution fusion | flops 402653184 | bytes 10493952 | tf_op jit(solution)/shard_map/shc,jksi->hjkci/dot_general | solution.py:26
  20.0 0.2 copy.42
  20.2 1.1 %copy-done.1 = f32[64,16,16,256]{3,0,2,1:T(8,128)} copy-done((f32[64,16,16,256]{3,0,2,1:T(8,128)}, f32[64,16,16,256]{3,0,2,1:T(8,128)S(1)}, u32[]{:S(2)}) %copy-start.1) | copy-done | bytes 16777240
  21.3 0.0 copy-done
  21.3 0.0 copy-start.3
  21.3 2.2 %convolution_bitcast_fusion = f32[64,2048]{1,0:T(8,128)S(1)} fusion(f32[2048,256]{1,0:T(8,128)S(1)} %bitcast.84, f32[256,64]{0,1:T(8,128)S(1)} %copy-done), kind=kOutput, calls=%fused_computation.5 | convolution fusion | flops 402653184 | bytes 2686976 | tf_op jit(solution)/shard_map/dot_general | solution.py:27
  23.4 0.1 reshape.44
  23.5 0.2 copy.43
  23.7 0.0 copy-done.3
  23.8 0.2 maximum_bitcast_fusion.1
  24.0 1.5 %copy.44 = f32[128,1,1088]{2,1,0:T(1,128)} copy(f32[128,1,1088]{0,2,1:T(8,128)S(1)} %maximum_bitcast_fusion.1) | data formatting | bytes 1114112 | tf_op jit(solution)/shard_map/all_to_all | solution.py:35
  25.5 11.5 %all-to-all-start.1 = ((f32[128,1,1088]{2,1,0:T(1,128)}), f32[128,1,1088]{2,1,0:T(1,128)S(1)}, u32[]{:S(2)}, u32[]{:S(2)}) async-start(f32[128,1,1088]{2,1,0:T(1,128)} %copy.44), calls=%async_computation.1 | async-start | bytes 1179648 | tf_op jit(solution)/shard_map/all_to_all | solution.py:35
  37.0 6.8 %fusion.2 = f32[2,8,16,8,256]{4,3,0,2,1:T(8,128)S(1)} fusion(f32[16,16,64,256]{3,2,1,0:T(8,128)} %bitcast.83, f32[64,16]{0,1:T(8,128)S(1)} %copy-done.2), kind=kOutput, calls=%fused_computation.7 | convolution fusion | flops 402653184 | bytes 10489856 | tf_op jit(solution)/shard_map/shc,jksi->hjkci/dot_general | solution.py:26
  43.8 0.2 copy.36
  44.1 2.2 %convolution_bitcast_fusion.1 = f32[64,2048]{1,0:T(8,128)S(1)} fusion(f32[2048,256]{1,0:T(8,128)S(1)} %bitcast.85, f32[256,64]{0,1:T(8,128)S(1)} %copy-done), kind=kOutput, calls=%fused_computation.6 | convolution fusion | flops 402653184 | bytes 2686976 | tf_op jit(solution)/shard_map/dot_general | solution.py:27
  46.2 0.1 reshape.40
  46.3 0.2 copy.37
  46.5 0.2 maximum_bitcast_fusion
  46.7 1.5 %copy.38 = f32[128,1,1088]{2,1,0:T(1,128)} copy(f32[128,1,1088]{0,2,1:T(8,128)S(1)} %maximum_bitcast_fusion) | data formatting | bytes 1114112 | tf_op jit(solution)/shard_map/all_to_all | solution.py:35
  48.3 3.5 %all-to-all-done.1 = f32[128,1,1088]{2,1,0:T(1,128)S(1)} async-done(((f32[128,1,1088]{2,1,0:T(1,128)}), f32[128,1,1088]{2,1,0:T(1,128)S(1)}, u32[]{:S(2)}, u32[]{:S(2)}) %all-to-all-start.1) | async-done | bytes 557088 | tf_op jit(solution)/shard_map/all_to_all | solution.py:35
  51.7 6.3 %all-to-all-start = ((f32[128,1,1088]{2,1,0:T(1,128)}), f32[128,1,1088]{2,1,0:T(1,128)S(1)}, u32[]{:S(2)}, u32[]{:S(2)}) async-start(f32[128,1,1088]{2,1,0:T(1,128)} %copy.38), calls=%async_computation | async-start | bytes 1179648 | tf_op jit(solution)/shard_map/all_to_all | solution.py:35
  58.0 0.9 copy.45
  59.0 13.7 %all-to-all-done = f32[128,1,1088]{2,1,0:T(1,128)S(1)} async-done(((f32[128,1,1088]{2,1,0:T(1,128)}), f32[128,1,1088]{2,1,0:T(1,128)S(1)}, u32[]{:S(2)}, u32[]{:S(2)}) %all-to-all-start) | async-done | bytes 557088 | tf_op jit(solution)/shard_map/all_to_all | solution.py:35
  72.7 0.9 copy.39
  73.7 0.2 copy.46
  73.9 0.1 copy.47
  74.0 0.2 copy.40
  74.2 0.1 copy.41
  74.3 0.5 convolution_bitcast_fusion.2
  74.8 0.5 fusion.4
  75.3 0.2 copy.48
  75.5 0.1 dot_general.35
  75.6 0.1 reshape.55
  75.8 0.4 fusion.14
  76.2 7.6 %all_to_all.34 = f32[8,16,128]{2,1,0:T(8,128)S(1)} all-to-all(f32[8,16,128]{2,1,0:T(8,128)S(1)} %fusion.14), channel_id=1, replica_groups=mesh['wa'=16,'an'=8] {'an'}, dimensions={0} | all-to-all | bytes 131072 | tf_op jit(solution)/shard_map/all_to_all | solution.py:43
  83.8 12.7 %all_to_all.35 = f32[16,16,128]{2,1,0:T(8,128)S(1)} all-to-all(f32[16,16,128]{2,1,0:T(8,128)S(1)} %broadcast_in_dim.24), channel_id=1, replica_groups=mesh['wa'=16,'an'=8] {'wa'}, dimensions={0} | all-to-all | bytes 262144 | tf_op jit(solution)/shard_map/all_to_all | solution.py:46
  96.5 0.6 broadcast_multiply_fusion
  (11 shorter events, 0.1 us)
Async XLA Ops:
  0.0 21.3 %copy-start = (f32[256,64]{0,1:T(8,128)S(1)}, f32[256,64]{0,1:T(8,128)}, u32[]{:S(2)}) copy-start(f32[256,64]{0,1:T(8,128)} %param.5) | copy-start | bytes 196612
  0.0 15.6 %copy-start.2 = (f32[64,16]{0,1:T(8,128)S(1)}, f32[64,16]{0,1:T(8,128)}, u32[]{:S(2)}) copy-start(f32[64,16]{0,1:T(8,128)} %param.7) | copy-start | bytes 12292
  15.6 5.7 %copy-start.1 = (f32[64,16,16,256]{3,0,2,1:T(8,128)}, f32[64,16,16,256]{3,0,2,1:T(8,128)S(1)}, u32[]{:S(2)}) copy-start(f32[64,16,16,256]{3,0,2,1:T(8,128)S(1)} %copy.66) | copy-start | bytes 50331652
  21.3 2.4 %copy-start.3 = (f32[16,64]{1,0:T(8,128)S(1)}, f32[16,64]{1,0:T(8,128)}, u32[]{:S(2)}) copy-start(f32[16,64]{1,0:T(8,128)} %param.6) | copy-start | bytes 12292
  25.5 26.2 %all-to-all-start.1 = ((f32[128,1,1088]{2,1,0:T(1,128)}), f32[128,1,1088]{2,1,0:T(1,128)S(1)}, u32[]{:S(2)}, u32[]{:S(2)}) async-start(f32[128,1,1088]{2,1,0:T(1,128)} %copy.44), calls=%async_computation.1 | async-start | bytes 1179648 | tf_op jit(solution)/shard_map/all_to_all | solution.py:35
  51.7 21.0 %all-to-all-start = ((f32[128,1,1088]{2,1,0:T(1,128)}), f32[128,1,1088]{2,1,0:T(1,128)S(1)}, u32[]{:S(2)}, u32[]{:S(2)}) async-start(f32[128,1,1088]{2,1,0:T(1,128)} %copy.38), calls=%async_computation | async-start | bytes 1179648 | tf_op jit(solution)/shard_map/all_to_all | solution.py:35

commit v8 on v6

--- a/solution.py
+++ b/solution.py
@@ -38,14 +38,14 @@
     gathered = payload[:, :block].reshape(fibre_parts, slab_parts, fibre_cells, slab_cells * columns)
     projected = jnp.einsum("wajx,wjp->axp", gathered, whole_two, precision=highest)
     projected = projected.reshape(slab_parts * slab_cells, columns * rank_two)
-    partial_gram = jnp.dot(projected, projected.T, precision=highest)
+    partial_gram = jnp.dot(projected, projected.T, precision=highest) / (rank_one * rank_two * rank_four)
     row_blocks = partial_gram.reshape(slab_parts, slab_cells, slab_parts * slab_cells)
     row_blocks = lax.all_to_all(row_blocks, "an", 0, 0, tiled=True)
     gram_rows = jnp.sum(row_blocks, axis=0)
     gram_rows = jnp.broadcast_to(gram_rows[None], (fibre_parts,) + gram_rows.shape)
     gram_rows = lax.all_to_all(gram_rows, "wa", 0, 0, tiled=True)
     gram_rows = jnp.sum(gram_rows, axis=0)
-    return gram_rows / (rank_one * rank_two * rank_four)
+    return gram_rows
 
 
 def solution(mesh):

time: 83.5 us -> 83.4 us (level)
  no operation moved by 1% of the time
where the time goes in v8:
time: 83.4 us; the launch traced here: 83.2 us
  blocking collectives  51.7 us (62%)
  matrix products  28.7 us (34%)
  local copies, waits for them, and re-layouts  1.99 us (2%)
    all_to_all x1, blocking collectives, on_device(): payload = lax.all_to_all(payload, ('wa', 'an'), 0, 0, tiled=True)  31.4 us
    dot_general x1, matrix products, on_device(): jnp.einsum('shc,sjki->hjkci', factor_four.reshape(species_count, halves,...  22.3 us
    all_to_all x1, blocking collectives, on_device(): gram_rows = lax.all_to_all(gram_rows, 'wa', 0, 0, tiled=True)  12.7 us
    all_to_all x1, blocking collectives, on_device(): row_blocks = lax.all_to_all(row_blocks, 'an', 0, 0, tiled=True)  7.58 us
    dot_general x1, matrix products, on_device(): lax.dot_general(factor_one, reduced.reshape(-1, first_cells), (((0,), (1,...  4.19 us
    dot_general x1, matrix products, on_device(): jnp.einsum('wajx,wjp->axp', gathered, whole_two, precision=highest)  1.81 us

profile of v8, /device:TPU:1, one launch (start us, length us, event | category | flops | bytes accessed | tf_op | source)
XLA Modules:
  0.0 83.2 jit_solution(6178405128397727470)
XLA Ops:
  0.0 0.0 copy-start
  0.0 22.3 %fusion.2 = f32[2,16,16,8,256]{4,3,0,2,1:T(8,128)S(1)} fusion(f32[64,16,16,256,1]{3,2,1,0,4:T(8,128)} %bitcast.34, f32[64,16]{0,1:T(8,128)} %param.7), kind=kOutput, calls=%fused_computation.3 | convolution fusion | flops 805306368 | bytes 20975616 | tf_op jit(solution)/shard_map/shc,sjki->hjkci/dot_general | solution.py:18
  22.3 0.6 copy.15
  22.9 0.0 copy-start.1
  22.9 0.0 copy-done
  22.9 4.2 %convolution_bitcast_fusion = f32[64,4096]{1,0:T(8,128)S(1)} fusion(f32[4096,256]{1,0:T(8,128)S(1)} %bitcast.35, f32[256,64]{0,1:T(8,128)S(1)} %copy-done), kind=kOutput, calls=%fused_computation.2 | convolution fusion | flops 805306368 | bytes 5308416 | tf_op jit(solution)/shard_map/dot_general | solution.py:24
  27.1 0.2 reshape.29
  27.3 0.0 copy-done.1
  27.3 0.1 reshape.30
  27.4 0.1 pad_maximum_fusion
  27.4 0.8 all_to_all.14
  28.2 31.4 %all_to_all.22 = f32[128,1,2176]{2,1,0:T(1,128)S(1)} all-to-all(f32[128,1,2176]{2,1,0:T(1,128)S(1)} %all_to_all.14), channel_id=1, replica_groups=mesh['wa'=16,'an'=8] {'wa','an'}, dimensions={0} | all-to-all | bytes 2228224 | tf_op jit(solution)/shard_map/all_to_all | solution.py:36
  59.6 0.1 copy.35
  59.7 0.1 slice_bitcast_fusion
  59.8 0.1 reshape.37
  59.9 1.8 %convolution_bitcast_fusion.1 = f32[8,128,64]{2,1,0:T(8,128)S(1)} fusion(f32[16,8,16,128]{3,1,2,0:T(8,128)S(1)} %slice_bitcast_fusion, f32[16,16,64,1]{2,1,0,3:T(8,128)S(1)} %reshape.37), kind=kOutput, calls=%fused_computation.4 | convolution fusion | flops 201326592 | bytes 1376256 | tf_op jit(solution)/shard_map/wajx,wjp->axp/dot_general | solution.py:39
  61.7 0.1 reshape.33
  61.9 0.4 convolution_multiply_fusion
  62.3 7.6 %all_to_all.23 = f32[8,16,128]{2,1,0:T(8,128)S(1)} all-to-all(f32[8,16,128]{2,1,0:T(8,128)S(1)} %bitcast.38), channel_id=1, replica_groups=mesh['wa'=16,'an'=8] {'an'}, dimensions={0} | all-to-all | bytes 131072 | tf_op jit(solution)/shard_map/all_to_all | solution.py:43
  69.9 12.7 %all_to_all.24 = f32[16,16,128]{2,1,0:T(8,128)S(1)} all-to-all(f32[16,16,128]{2,1,0:T(8,128)S(1)} %broadcast_in_dim.15), channel_id=1, replica_groups=mesh['wa'=16,'an'=8] {'wa'}, dimensions={0} | all-to-all | bytes 262144 | tf_op jit(solution)/shard_map/all_to_all | solution.py:46
  82.6 0.6 reduce_sum.19
  (5 shorter events, 0.0 us)
Async XLA Ops:
  0.0 22.9 %copy-start = (f32[256,64]{0,1:T(8,128)S(1)}, f32[256,64]{0,1:T(8,128)}, u32[]{:S(2)}) copy-start(f32[256,64]{0,1:T(8,128)} %param.5) | copy-start | bytes 196612
  22.9 4.4 %copy-start.1 = (f32[16,64]{1,0:T(8,128)S(1)}, f32[16,64]{1,0:T(8,128)}, u32[]{:S(2)}) copy-start(f32[16,64]{1,0:T(8,128)} %param.6) | copy-start | bytes 12292

commit v9 on v6

--- a/solution.py
+++ b/solution.py
@@ -33,9 +33,10 @@
     own_two = factor_two.reshape(slab_parts, piece_len)
     piece = lax.dynamic_index_in_dim(own_two, lax.axis_index("an"), 0, keepdims=True)
     payload = jnp.concatenate([mixed, jnp.broadcast_to(piece, (devices, piece_len))], axis=1)
-    payload = lax.all_to_all(payload, ("wa", "an"), 0, 0, tiled=True)
-    whole_two = payload[:, block:].reshape(fibre_parts, fibre_cells, rank_two)
-    gathered = payload[:, :block].reshape(fibre_parts, slab_parts, fibre_cells, slab_cells * columns)
+    payload = lax.all_to_all(payload, ("an", "wa"), 0, 0, tiled=True)
+    payload = payload.reshape(slab_parts, fibre_parts, block + piece_len).transpose(1, 0, 2)
+    whole_two = payload[:, :, block:].reshape(fibre_parts, fibre_cells, rank_two)
+    gathered = payload[:, :, :block].reshape(fibre_parts, slab_parts, fibre_cells, slab_cells * columns)
     projected = jnp.einsum("wajx,wjp->axp", gathered, whole_two, precision=highest)
     projected = projected.reshape(slab_parts * slab_cells, columns * rank_two)
     partial_gram = jnp.dot(projected, projected.T, precision=highest)

time: 83.5 us -> 84.2 us (level)
  no operation moved by 1% of the time
where the time goes in v9:
time: 84.2 us; the launch traced here: 84 us
  blocking collectives  52.1 us (62%)
  matrix products  28.7 us (34%)
  local copies, waits for them, and re-layouts  2.34 us (3%)
    all_to_all x1, blocking collectives, on_device(): payload = lax.all_to_all(payload, ('an', 'wa'), 0, 0, tiled=True)  31.1 us
    dot_general x1, matrix products, on_device(): jnp.einsum('shc,sjki->hjkci', factor_four.reshape(species_count, halves,...  22.3 us
    all_to_all x1, blocking collectives, on_device(): gram_rows = lax.all_to_all(gram_rows, 'wa', 0, 0, tiled=True)  13.4 us
    all_to_all x1, blocking collectives, on_device(): row_blocks = lax.all_to_all(row_blocks, 'an', 0, 0, tiled=True)  7.58 us
    dot_general x1, matrix products, on_device(): lax.dot_general(factor_one, reduced.reshape(-1, first_cells), (((0,), (1,...  4.19 us
    dot_general x1, matrix products, on_device(): jnp.einsum('wajx,wjp->axp', gathered, whole_two, precision=highest)  1.81 us

profile of v9, /device:TPU:1, one launch (start us, length us, event | category | flops | bytes accessed | tf_op | source)
XLA Modules:
  0.0 84.0 jit_solution(11361578203364514889)
XLA Ops:
  0.0 0.0 copy-start
  0.0 22.3 %fusion.2 = f32[2,16,16,8,256]{4,3,0,2,1:T(8,128)S(1)} fusion(f32[64,16,16,256,1]{3,2,1,0,4:T(8,128)} %bitcast.39, f32[64,16]{0,1:T(8,128)} %param.7), kind=kOutput, calls=%fused_computation.3 | convolution fusion | flops 805306368 | bytes 20975616 | tf_op jit(solution)/shard_map/shc,sjki->hjkci/dot_general | solution.py:18
  22.3 0.6 copy.25
  22.9 0.0 copy-start.1
  22.9 0.0 copy-done
  22.9 4.2 %convolution_bitcast_fusion = f32[64,4096]{1,0:T(8,128)S(1)} fusion(f32[4096,256]{1,0:T(8,128)S(1)} %bitcast.40, f32[256,64]{0,1:T(8,128)S(1)} %copy-done), kind=kOutput, calls=%fused_computation.2 | convolution fusion | flops 805306368 | bytes 5308416 | tf_op jit(solution)/shard_map/dot_general | solution.py:24
  27.1 0.2 reshape.33
  27.3 0.0 copy-done.1
  27.3 0.1 reshape.34
  27.4 0.1 pad_maximum_fusion
  27.4 0.8 all_to_all.12
  28.2 31.1 %all_to_all.19 = f32[128,1,2176]{2,1,0:T(1,128)S(1)} all-to-all(f32[128,1,2176]{2,1,0:T(1,128)S(1)} %all_to_all.12), channel_id=1, replica_groups=mesh['wa'=16,'an'=8] {'an','wa'}, dimensions={0} | all-to-all | bytes 2228224 | tf_op jit(solution)/shard_map/all_to_all | solution.py:36
  59.3 0.1 copy.39
  59.4 0.1 slice.8
  59.5 0.2 copy.40
  59.7 0.1 reshape.41
  59.8 1.8 %convolution_bitcast_fusion.1 = f32[8,128,64]{2,1,0:T(8,128)S(1)} fusion(f32[16,8,16,128]{3,2,0,1:T(8,128)S(1)} %bitcast.44, f32[16,16,64,1]{2,1,0,3:T(8,128)S(1)} %reshape.41), kind=kOutput, calls=%fused_computation.4 | convolution fusion | flops 201326592 | bytes 1376256 | tf_op jit(solution)/shard_map/wajx,wjp->axp/dot_general | solution.py:40
  61.6 0.1 dot_general.20
  61.8 0.1 reshape.43
  61.9 0.4 fusion.6
  62.3 7.6 %all_to_all.20 = f32[8,16,128]{2,1,0:T(8,128)S(1)} all-to-all(f32[8,16,128]{2,1,0:T(8,128)S(1)} %fusion.6), channel_id=1, replica_groups=mesh['wa'=16,'an'=8] {'an'}, dimensions={0} | all-to-all | bytes 131072 | tf_op jit(solution)/shard_map/all_to_all | solution.py:44
  69.9 13.4 %all_to_all.21 = f32[16,16,128]{2,1,0:T(8,128)S(1)} all-to-all(f32[16,16,128]{2,1,0:T(8,128)S(1)} %broadcast_in_dim.15), channel_id=1, replica_groups=mesh['wa'=16,'an'=8] {'wa'}, dimensions={0} | all-to-all | bytes 262144 | tf_op jit(solution)/shard_map/all_to_all | solution.py:47
  83.4 0.6 broadcast_multiply_fusion
  (7 shorter events, 0.1 us)
Async XLA Ops:
  0.0 22.9 %copy-start = (f32[256,64]{0,1:T(8,128)S(1)}, f32[256,64]{0,1:T(8,128)}, u32[]{:S(2)}) copy-start(f32[256,64]{0,1:T(8,128)} %param.5) | copy-start | bytes 196612
  22.9 4.4 %copy-start.1 = (f32[16,64]{1,0:T(8,128)S(1)}, f32[16,64]{1,0:T(8,128)}, u32[]{:S(2)}) copy-start(f32[16,64]{1,0:T(8,128)} %param.6) | copy-start | bytes 12292

commit v10 on v6

--- a/solution.py
+++ b/solution.py
@@ -1,7 +1,40 @@
 import jax
 import jax.numpy as jnp
 from jax import lax
+from jax.experimental import pallas as pl
 from jax.sharding import PartitionSpec as P
+
+
+def species_kernel(weights_ref, field_ref, out_ref):
+    weights = weights_ref[...]
+    rows = weights.shape[1] // field_ref.shape[0]
+    for part in range(field_ref.shape[2] // rows):
+        block = field_ref[:, 0, part * rows:(part + 1) * rows, :].reshape(weights.shape[1], field_ref.shape[3])
+        out = jnp.dot(weights, block, precision=lax.Precision.HIGHEST, preferred_element_type=jnp.float32)
+        out_ref[:, 0, part * rows:(part + 1) * rows] = out.reshape(
+            out_ref.shape[0], rows, out_ref.shape[3], out_ref.shape[4]
+        )
+
+
+def reduce_species(mass_field, factor_four, columns, rows):
+    species_count, fibre_cells, slab_cells, first_cells = mass_field.shape
+    rank_four = factor_four.shape[1]
+    halves = rank_four // columns
+    weights = factor_four.reshape(species_count, halves, 1, columns, 1).transpose(1, 2, 3, 0, 4)
+    weights = weights * jnp.eye(rows, dtype=factor_four.dtype).reshape(1, rows, 1, 1, rows)
+    weights = weights.reshape(rank_four * rows, species_count * rows)
+    return pl.pallas_call(
+        species_kernel,
+        grid=(fibre_cells,),
+        in_specs=[
+            pl.BlockSpec((rank_four * rows, species_count * rows), lambda g: (0, 0)),
+            pl.BlockSpec((species_count, 1, slab_cells, first_cells), lambda g: (0, g, 0, 0)),
+        ],
+        out_specs=pl.BlockSpec((halves, 1, slab_cells, columns, first_cells), lambda g: (0, g, 0, 0, 0)),
+        out_shape=jax.ShapeDtypeStruct(
+            (halves, fibre_cells, slab_cells, columns, first_cells), jnp.float32
+        ),
+    )(weights, mass_field)
 
 
 def on_device(mass_field, factor_one, factor_two, factor_four):
@@ -15,12 +48,7 @@
     devices = fibre_parts * slab_parts
     columns = rank_one * rank_four // devices
     halves = rank_four // columns
-    reduced = jnp.einsum(
-        "shc,sjki->hjkci",
-        factor_four.reshape(species_count, halves, columns),
-        mass_field,
-        precision=highest,
-    )
+    reduced = reduce_species(mass_field, factor_four, columns, 4)
     mixed = lax.dot_general(
         factor_one,
         reduced.reshape(-1, first_cells),

time: 83.5 us -> 85.2 us (1.020)
  matrix products: 28.7 us -> 8.52 us
  Pallas kernels: 0 us -> 18.8 us
  local copies, waits for them, and re-layouts: 2.13 us -> 4.3 us
    dot_general x1 -> x0, matrix products: 22.3 us -> none  [on_device(): jnp.einsum('shc,sjki->hjkci', factor_four.reshape(species_count, halves,...]
    pallas_call x0 -> x1, Pallas kernels: none -> 18.8 us  [reduce_species(): pl.pallas_call(species_kernel, grid=(fibre_cells,), in_specs=[pl.BlockSpe...]
    mul x0 -> x3, local copies, waits for them, and re-layouts: none -> 2.22 us  [reduce_species(): weights * jnp.eye(rows, dtype=factor_four.dtype).reshape(1, rows, 1, 1, r...]
    dot_general x1, matrix products: 4.19 us -> 6.34 us  [on_device(): lax.dot_general(factor_one, reduced.reshape(-1, first_cells), (((0,), (1,...]
where the time goes in v10:
time: 85.2 us; the launch traced here: 84.5 us
  blocking collectives  51.7 us (61%)
  Pallas kernels  18.8 us (22%)
  matrix products  8.52 us (10%)
  local copies, waits for them, and re-layouts  4.3 us (5%)
  other arithmetic  1.04 us (1%)
    all_to_all x1, blocking collectives, on_device(): payload = lax.all_to_all(payload, ('wa', 'an'), 0, 0, tiled=True)  31.4 us
    pallas_call x1, Pallas kernels, reduce_species(): pl.pallas_call(species_kernel, grid=(fibre_cells,), in_specs=[pl.BlockSpe...  18.8 us
    all_to_all x1, blocking collectives, on_device(): gram_rows = lax.all_to_all(gram_rows, 'wa', 0, 0, tiled=True)  12.7 us
    all_to_all x1, blocking collectives, on_device(): row_blocks = lax.all_to_all(row_blocks, 'an', 0, 0, tiled=True)  7.58 us
    dot_general x1, matrix products, on_device(): lax.dot_general(factor_one, reduced.reshape(-1, first_cells), (((0,), (1,...  6.34 us
    mul x3, local copies, waits for them, and re-layouts, reduce_species(): weights * jnp.eye(rows, dtype=factor_four.dtype).reshape(1, rows, 1, 1, r...  2.22 us
    dot_general x1, matrix products, on_device(): jnp.einsum('wajx,wjp->axp', gathered, whole_two, precision=highest)  1.81 us

profile of v10, /device:TPU:1, one launch (start us, length us, event | category | flops | bytes accessed | tf_op | source)
XLA Modules:
  0.0 84.5 jit_solution(4155345518751856839)
XLA Ops:
  0.0 0.0 copy-start
  0.0 0.8 copy.15
  0.8 0.3 broadcast_multiply_fusion
  1.2 0.7 mul.23
  1.9 0.7 copy.16.weights_ref
  2.6 18.8 %shard_map.46 = f32[2,16,16,8,256]{4,3,2,1,0:T(8,128)} custom-call(f32[64,256]{1,0:T(8,128)} %copy.16.weights_ref, f32[64,16,16,256]{3,2,1,0:T(8,128)} %field_ref.1), custom_call_target="tpu_custom_call" | custom-call | tf_op jit(solution)/shard_map/pallas_call | solution.py:26
  21.4 0.0 copy-done
  21.4 6.3 %convolution_bitcast_fusion = f32[64,4096]{1,0:T(8,128)S(1)} fusion(f32[4096,256]{1,0:T(8,128)} %bitcast.32, f32[256,64]{0,1:T(8,128)S(1)} %copy-done), kind=kOutput, calls=%fused_computation | convolution fusion | flops 805306368 | bytes 5308416 | tf_op jit(solution)/shard_map/dot_general | solution.py:52
  27.7 0.0 copy-start.1
  27.7 0.2 reshape.42
  27.9 0.5 copy-done.1
  28.4 0.1 reshape.43
  28.5 0.1 pad_maximum_fusion
  28.6 0.8 all_to_all.14
  29.4 31.4 %all_to_all.22 = f32[128,1,2176]{2,1,0:T(1,128)S(1)} all-to-all(f32[128,1,2176]{2,1,0:T(1,128)S(1)} %all_to_all.14), channel_id=1, replica_groups=mesh['wa'=16,'an'=8] {'wa','an'}, dimensions={0} | all-to-all | bytes 2228224 | tf_op jit(solution)/shard_map/all_to_all | solution.py:64
  60.8 0.1 copy.30
  60.8 0.1 slice_bitcast_fusion
  61.0 0.1 reshape.47
  61.0 1.8 %convolution_bitcast_fusion.1 = f32[8,128,64]{2,1,0:T(8,128)S(1)} fusion(f32[16,8,16,128]{3,1,2,0:T(8,128)S(1)} %slice_bitcast_fusion, f32[16,16,64,1]{2,1,0,3:T(8,128)S(1)} %reshape.47), kind=kOutput, calls=%fused_computation.1 | convolution fusion | flops 201326592 | bytes 1376256 | tf_op jit(solution)/shard_map/wajx,wjp->axp/dot_general | solution.py:67
  62.9 0.1 dot_general.16
  63.0 0.1 reshape.49
  63.2 0.4 fusion.4
  63.5 7.6 %all_to_all.23 = f32[8,16,128]{2,1,0:T(8,128)S(1)} all-to-all(f32[8,16,128]{2,1,0:T(8,128)S(1)} %fusion.4), channel_id=1, replica_groups=mesh['wa'=16,'an'=8] {'an'}, dimensions={0} | all-to-all | bytes 131072 | tf_op jit(solution)/shard_map/all_to_all | solution.py:71
  71.1 12.7 %all_to_all.24 = f32[16,16,128]{2,1,0:T(8,128)S(1)} all-to-all(f32[16,16,128]{2,1,0:T(8,128)S(1)} %broadcast_in_dim.15), channel_id=1, replica_groups=mesh['wa'=16,'an'=8] {'wa'}, dimensions={0} | all-to-all | bytes 262144 | tf_op jit(solution)/shard_map/all_to_all | solution.py:74
  83.9 0.6 broadcast_multiply_fusion.1
  (7 shorter events, 0.1 us)
Async XLA Ops:
  0.0 21.4 %copy-start = (f32[256,64]{0,1:T(8,128)S(1)}, f32[256,64]{0,1:T(8,128)}, u32[]{:S(2)}) copy-start(f32[256,64]{0,1:T(8,128)} %param.5) | copy-start | bytes 196612
  27.7 0.7 copy-start.1

commit v11 on v6

--- a/solution.py
+++ b/solution.py
@@ -42,8 +42,10 @@
     row_blocks = partial_gram.reshape(slab_parts, slab_cells, slab_parts * slab_cells)
     row_blocks = lax.all_to_all(row_blocks, "an", 0, 0, tiled=True)
     gram_rows = jnp.sum(row_blocks, axis=0)
-    gram_rows = jnp.broadcast_to(gram_rows[None], (fibre_parts,) + gram_rows.shape)
-    gram_rows = lax.all_to_all(gram_rows, "wa", 0, 0, tiled=True)
+    gram_rows = gram_rows + lax.ppermute(gram_rows, "wa", [(i, i ^ 1) for i in range(fibre_parts)])
+    groups = [list(range(core, fibre_parts, 2)) for core in range(2)]
+    gram_rows = jnp.broadcast_to(gram_rows[None], (fibre_parts // 2,) + gram_rows.shape)
+    gram_rows = lax.all_to_all(gram_rows, "wa", 0, 0, axis_index_groups=groups, tiled=True)
     gram_rows = jnp.sum(gram_rows, axis=0)
     return gram_rows / (rank_one * rank_two * rank_four)
 

time: 83.5 us -> 83.5 us (level)
  blocking collectives: 51.7 us -> 48.5 us
  starting transfers between devices: 0 us -> 2.06 us
    all_to_all x1, blocking collectives: 12.7 us -> 9.47 us  [on_device(): lax.all_to_all(gram_rows, 'wa', 0, 0, axis_index_groups=groups, tiled=True)]
    ppermute x0 -> x1, starting transfers between devices: none -> 2.06 us  [on_device(): lax.ppermute(gram_rows, 'wa', [(i, i ^ 1) for i in range(fibre_parts)])]
  transfers between devices with their start and end apart: 0 -> 1, of which waited for: 0 -> 1; matrix products, arithmetic and copies ran while one was open for 0% -> 0% of each run, Pallas kernels for 0% -> 0%
where the time goes in v11:
time: 83.5 us; the launch traced here: 83 us
  blocking collectives  48.5 us (58%)
  matrix products  28.7 us (34%)
  local copies, waits for them, and re-layouts  2.13 us (3%)
  starting transfers between devices  2.06 us (2%)
    all_to_all x1, blocking collectives, on_device(): payload = lax.all_to_all(payload, ('wa', 'an'), 0, 0, tiled=True)  31.4 us
    dot_general x1, matrix products, on_device(): jnp.einsum('shc,sjki->hjkci', factor_four.reshape(species_count, halves,...  22.3 us
    all_to_all x1, blocking collectives, on_device(): lax.all_to_all(gram_rows, 'wa', 0, 0, axis_index_groups=groups, tiled=True)  9.47 us
    all_to_all x1, blocking collectives, on_device(): row_blocks = lax.all_to_all(row_blocks, 'an', 0, 0, tiled=True)  7.58 us
    dot_general x1, matrix products, on_device(): lax.dot_general(factor_one, reduced.reshape(-1, first_cells), (((0,), (1,...  4.19 us
    ppermute x1, starting transfers between devices, on_device(): lax.ppermute(gram_rows, 'wa', [(i, i ^ 1) for i in range(fibre_parts)])  2.06 us
    dot_general x1, matrix products, on_device(): jnp.einsum('wajx,wjp->axp', gathered, whole_two, precision=highest)  1.81 us
  transfers between devices with their start and end apart: 1, of which 1 were waited for; matrix products, arithmetic and copies ran while one was open for 0% of the time, Pallas kernels for 0%

profile of v11, /device:TPU:1, one launch (start us, length us, event | category | flops | bytes accessed | tf_op | source)
XLA Modules:
  0.0 83.0 jit_solution(16794709218384753797)
XLA Ops:
  0.0 0.0 copy-start
  0.0 22.3 %fusion.2 = f32[2,16,16,8,256]{4,3,0,2,1:T(8,128)S(1)} fusion(f32[64,16,16,256,1]{3,2,1,0,4:T(8,128)} %bitcast.35, f32[64,16]{0,1:T(8,128)} %param.7), kind=kOutput, calls=%fused_computation.3 | convolution fusion | flops 805306368 | bytes 20975616 | tf_op jit(solution)/shard_map/shc,sjki->hjkci/dot_general | solution.py:18
  22.3 0.6 copy.17
  22.9 0.0 copy-start.1
  22.9 0.0 copy-done
  22.9 4.2 %convolution_bitcast_fusion = f32[64,4096]{1,0:T(8,128)S(1)} fusion(f32[4096,256]{1,0:T(8,128)S(1)} %bitcast.36, f32[256,64]{0,1:T(8,128)S(1)} %copy-done), kind=kOutput, calls=%fused_computation.2 | convolution fusion | flops 805306368 | bytes 5308416 | tf_op jit(solution)/shard_map/dot_general | solution.py:24
  27.1 0.2 reshape.29
  27.3 0.0 copy-done.1
  27.3 0.1 reshape.30
  27.4 0.1 pad_maximum_fusion
  27.4 0.8 all_to_all.14
  28.2 31.4 %all_to_all.22 = f32[128,1,2176]{2,1,0:T(1,128)S(1)} all-to-all(f32[128,1,2176]{2,1,0:T(1,128)S(1)} %all_to_all.14), channel_id=1, replica_groups=mesh['wa'=16,'an'=8] {'wa','an'}, dimensions={0} | all-to-all | bytes 2228224 | tf_op jit(solution)/shard_map/all_to_all | solution.py:36
  59.6 0.1 copy.39
  59.7 0.1 slice_bitcast_fusion
  59.8 0.1 reshape.36
  59.9 1.8 %convolution_bitcast_fusion.1 = f32[8,128,64]{2,1,0:T(8,128)S(1)} fusion(f32[16,8,16,128]{3,1,2,0:T(8,128)S(1)} %slice_bitcast_fusion, f32[16,16,64,1]{2,1,0,3:T(8,128)S(1)} %reshape.36), kind=kOutput, calls=%fused_computation.4 | convolution fusion | flops 201326592 | bytes 1376256 | tf_op jit(solution)/shard_map/wajx,wjp->axp/dot_general | solution.py:39
  61.7 0.1 dot_general.20
  61.9 0.1 reshape.38
  62.0 0.4 fusion.9
  62.4 7.6 %all_to_all.23 = f32[8,16,128]{2,1,0:T(8,128)S(1)} all-to-all(f32[8,16,128]{2,1,0:T(8,128)S(1)} %fusion.9), channel_id=1, replica_groups=mesh['wa'=16,'an'=8] {'an'}, dimensions={0} | all-to-all | bytes 131072 | tf_op jit(solution)/shard_map/all_to_all | solution.py:43
  70.0 2.1 %collective-permute-start = (f32[16,128]{1,0:T(8,128)S(1)}, f32[16,128]{1,0:T(8,128)S(1)}, u32[]{:S(2)}, u32[]{:S(2)}) collective-permute-start(f32[16,128]{1,0:T(8,128)S(1)} %reduce_sum.18), channel_id=1, source_target_pairs={{0,8},{8,0},{16,24},{24,16},{32,40},{40,32},{48,56},{56,48},{64,72... | collective-permute-start | bytes 24584 | tf_op jit(solution)/shard_map/ppermute | solution.py:45
  72.0 0.8 collective-permute-done
  72.9 9.5 %all_to_all.24 = f32[8,16,128]{2,1,0:T(8,128)S(1)} all-to-all(f32[8,16,128]{2,1,0:T(8,128)S(1)} %broadcast_in_dim.15), channel_id=1, replica_groups={{0,16,32,48,64,80,96,112},{8,24,40,56,72,88,104,120},{1,17,33,49,65,81,..., dimensions={0} | all-to-all | bytes 131072 | tf_op jit(solution)/shard_map/all_to_all | solution.py:48
  82.4 0.6 broadcast_multiply_fusion
  (7 shorter events, 0.1 us)
Async XLA Ops:
  0.0 22.9 %copy-start = (f32[256,64]{0,1:T(8,128)S(1)}, f32[256,64]{0,1:T(8,128)}, u32[]{:S(2)}) copy-start(f32[256,64]{0,1:T(8,128)} %param.5) | copy-start | bytes 196612
  22.9 4.4 %copy-start.1 = (f32[16,64]{1,0:T(8,128)S(1)}, f32[16,64]{1,0:T(8,128)}, u32[]{:S(2)}) copy-start(f32[16,64]{1,0:T(8,128)} %param.6) | copy-start | bytes 12292
  70.0 2.9 %collective-permute-start = (f32[16,128]{1,0:T(8,128)S(1)}, f32[16,128]{1,0:T(8,128)S(1)}, u32[]{:S(2)}, u32[]{:S(2)}) collective-permute-start(f32[16,128]{1,0:T(8,128)S(1)} %reduce_sum.18), channel_id=1, source_target_pairs={{0,8},{8,0},{16,24},{24,16},{32,40},{40,32},{48,56},{56,48},{64,72... | collective-permute-start | bytes 24584 | tf_op jit(solution)/shard_map/ppermute | solution.py:45

commit v12 on v6

--- a/solution.py
+++ b/solution.py
@@ -32,8 +32,10 @@
     piece_len = fibre_cells * rank_two // slab_parts
     own_two = factor_two.reshape(slab_parts, piece_len)
     piece = lax.dynamic_index_in_dim(own_two, lax.axis_index("an"), 0, keepdims=True)
-    payload = jnp.concatenate([mixed, jnp.broadcast_to(piece, (devices, piece_len))], axis=1)
-    payload = lax.all_to_all(payload, ("wa", "an"), 0, 0, tiled=True)
+    payload = jnp.concatenate(
+        [mixed[:, None, :], jnp.broadcast_to(piece[None], (devices, 1, piece_len))], axis=2
+    )
+    payload = lax.all_to_all(payload, ("wa", "an"), 0, 0, tiled=True).reshape(devices, -1)
     whole_two = payload[:, block:].reshape(fibre_parts, fibre_cells, rank_two)
     gathered = payload[:, :block].reshape(fibre_parts, slab_parts, fibre_cells, slab_cells * columns)
     projected = jnp.einsum("wajx,wjp->axp", gathered, whole_two, precision=highest)

time: 83.5 us -> 84.7 us (1.014)
  other arithmetic: 0.71 us -> 1.58 us
    another operation x0 -> x1, local copies, waits for them, and re-layouts: none -> 1.25 us  [on_device(): mixed[:, None, :]]
    concatenate x1, other arithmetic: 0.08 us -> 0.94 us  [on_device(): jnp.concatenate([mixed[:, None, :], jnp.broadcast_to(piece[None], (device...]
where the time goes in v12:
time: 84.7 us; the launch traced here: 84.5 us
  blocking collectives  51.7 us (61%)
  matrix products  28.7 us (34%)
  local copies, waits for them, and re-layouts  2.45 us (3%)
  other arithmetic  1.58 us (2%)
    all_to_all x1, blocking collectives, on_device(): lax.all_to_all(payload, ('wa', 'an'), 0, 0, tiled=True).reshape(devices, -1)  31.4 us
    dot_general x1, matrix products, on_device(): jnp.einsum('shc,sjki->hjkci', factor_four.reshape(species_count, halves,...  22.3 us
    all_to_all x1, blocking collectives, on_device(): gram_rows = lax.all_to_all(gram_rows, 'wa', 0, 0, tiled=True)  12.7 us
    all_to_all x1, blocking collectives, on_device(): row_blocks = lax.all_to_all(row_blocks, 'an', 0, 0, tiled=True)  7.58 us
    dot_general x1, matrix products, on_device(): lax.dot_general(factor_one, reduced.reshape(-1, first_cells), (((0,), (1,...  4.19 us
    dot_general x1, matrix products, on_device(): jnp.einsum('wajx,wjp->axp', gathered, whole_two, precision=highest)  1.81 us

profile of v12, /device:TPU:1, one launch (start us, length us, event | category | flops | bytes accessed | tf_op | source)
XLA Modules:
  0.0 84.5 jit_solution(4452543518480047185)
XLA Ops:
  0.0 0.0 copy-start
  0.0 22.3 %fusion.2 = f32[2,16,16,8,256]{4,3,0,2,1:T(8,128)S(1)} fusion(f32[64,16,16,256,1]{3,2,1,0,4:T(8,128)} %bitcast.35, f32[64,16]{0,1:T(8,128)} %param.7), kind=kOutput, calls=%fused_computation.3 | convolution fusion | flops 805306368 | bytes 20975616 | tf_op jit(solution)/shard_map/shc,sjki->hjkci/dot_general | solution.py:18
  22.3 0.6 copy.18
  22.9 0.0 copy-start.1
  22.9 0.0 copy-done
  22.9 4.2 %convolution_bitcast_fusion = f32[64,4096]{1,0:T(8,128)S(1)} fusion(f32[4096,256]{1,0:T(8,128)S(1)} %bitcast.36, f32[256,64]{0,1:T(8,128)S(1)} %copy-done), kind=kOutput, calls=%fused_computation.2 | convolution fusion | flops 805306368 | bytes 5308416 | tf_op jit(solution)/shard_map/dot_general | solution.py:24
  27.1 1.2 %broadcast_in_dim_reshape.4 = f32[128,1,2048]{2,1,0:T(1,128)S(1)} reshape(f32[64,4096]{1,0:T(8,128)S(1)} %convolution_bitcast_fusion) | data formatting | bytes 2097152 | tf_op jit(solution)/shard_map/broadcast_in_dim;reshape | solution.py:36
  28.4 0.0 copy-done.1
  28.4 0.1 reshape.30
  28.4 0.9 %pad_maximum_fusion = f32[128,1,2176]{2,1,0:T(1,128)S(1)} fusion(f32[128,1,2048]{2,1,0:T(1,128)S(1)} %broadcast_in_dim_reshape.4, f32[2176]{0:T(1024)S(1)} %pad.1.clone), kind=kLoop, calls=%fused_computation.5 | loop fusion | flops 278528 | bytes 2171392 | tf_op jit(solution)/shard_map/concatenate | solution.py:35
  29.4 31.4 %all_to_all.15 = f32[128,1,2176]{2,1,0:T(1,128)S(1)} all-to-all(f32[128,1,2176]{2,1,0:T(1,128)S(1)} %pad_maximum_fusion), channel_id=1, replica_groups=mesh['wa'=16,'an'=8] {'wa','an'}, dimensions={0} | all-to-all | bytes 2228224 | tf_op jit(solution)/shard_map/all_to_all | solution.py:38
  60.8 0.1 copy.41
  60.9 0.1 slice_bitcast_fusion
  61.0 0.1 reshape.37
  61.1 1.8 %convolution_bitcast_fusion.1 = f32[8,128,64]{2,1,0:T(8,128)S(1)} fusion(f32[16,8,16,128]{3,1,2,0:T(8,128)S(1)} %slice_bitcast_fusion, f32[16,16,64,1]{2,1,0,3:T(8,128)S(1)} %reshape.37), kind=kOutput, calls=%fused_computation.4 | convolution fusion | flops 201326592 | bytes 1376256 | tf_op jit(solution)/shard_map/wajx,wjp->axp/dot_general | solution.py:41
  62.9 0.1 dot_general.20
  63.0 0.1 reshape.39
  63.2 0.4 fusion.9
  63.6 7.6 %all_to_all.16 = f32[8,16,128]{2,1,0:T(8,128)S(1)} all-to-all(f32[8,16,128]{2,1,0:T(8,128)S(1)} %fusion.9), channel_id=1, replica_groups=mesh['wa'=16,'an'=8] {'an'}, dimensions={0} | all-to-all | bytes 131072 | tf_op jit(solution)/shard_map/all_to_all | solution.py:45
  71.2 12.7 %all_to_all.17 = f32[16,16,128]{2,1,0:T(8,128)S(1)} all-to-all(f32[16,16,128]{2,1,0:T(8,128)S(1)} %broadcast_in_dim.16), channel_id=1, replica_groups=mesh['wa'=16,'an'=8] {'wa'}, dimensions={0} | all-to-all | bytes 262144 | tf_op jit(solution)/shard_map/all_to_all | solution.py:48
  83.9 0.6 broadcast_multiply_fusion
  (6 shorter events, 0.1 us)
Async XLA Ops:
  0.0 22.9 %copy-start = (f32[256,64]{0,1:T(8,128)S(1)}, f32[256,64]{0,1:T(8,128)}, u32[]{:S(2)}) copy-start(f32[256,64]{0,1:T(8,128)} %param.5) | copy-start | bytes 196612
  22.9 5.5 %copy-start.1 = (f32[16,64]{1,0:T(8,128)S(1)}, f32[16,64]{1,0:T(8,128)}, u32[]{:S(2)}) copy-start(f32[16,64]{1,0:T(8,128)} %param.6) | copy-start | bytes 12292
